TPU v7x, 256 devices: a whole 4x4x8 slice. The times are simulated.
256 devices in a mesh: facet: 8 (over z), chan: 32 (over y, x, core).
Axes of the slice: x: 4, y: 4, z: 8, core: 2. Of those that a mesh axis runs over, the one named last changes fastest.
Arguments:
- sky_image: float32 [256, 32, 4096], P('chan', 'facet'), may hold values from -100 to 100
- dual_field: float32 [256, 32, 4096], P(None, 'facet', 'chan'), may hold values from -100 to 100
- sketch_matrix: bfloat16 [32, 4096, 128], P('facet', 'chan'), may hold values from -0.046875 to 0.046875
- grid_tiles: float32 [256, 4, 128, 128], P('chan'), may hold values from -0.5 to 0.5
- freq_block: int32 [256, 4], P('chan'), may hold values from 0 to 31
- vis_block: int32 [256, 4], P('chan'), may hold values from 0 to 3
- vis_data: float32 [256, 2, 32, 4, 128], P('chan', None, 'facet'), may hold values from -6 to 6
Outputs:
- new_image: float32 [256, 32, 4096], P('chan', 'facet')
- new_dual: float32 [256, 32, 4096], P(None, 'facet', 'chan')
All inputs are finite; a program needn't handle non-finite values.
Results may differ from a plain program's by a relative error of at most 0.0003.
Values sent between devices are 32-bit elements; how exact they have to be, the bound alone decides.
No kernel may reach another device: no remote copies, remote signals or barrier semaphores. Data moves between devices by JAX's collectives and lax.ppermute only.
A program may use at most 128 MiB of HBM per device.

v0:
```python
import math

import jax
import jax.numpy as jnp
from jax import lax
from jax.sharding import PartitionSpec as P

SIGN_ITERS = 12
ROOT_ITERS = 14


step_primal = 0.4
smooth_weight = 0.25
step_dual = 0.5
shrink_ratio = 0.25

HI = lax.Precision.HIGHEST


def padded_2(block, sides, width):
    for axis, dim in sides:
        count = lax.axis_size(axis)
        forward = [(i, i + 1) for i in range(count - 1)]
        backward = [(target, source) for source, target in forward]
        low = lax.ppermute(
            lax.slice_in_dim(block, block.shape[dim] - width, None, axis=dim), axis, forward
        )
        high = lax.ppermute(lax.slice_in_dim(block, 0, width, axis=dim), axis, backward)
        block = jnp.concatenate([low, block, high], axis=dim)
    return block


def matmul_hi(first_mat, second_mat):
    return jnp.dot(first_mat, second_mat, precision=HI)


def shrink_matrix(gram_mat):
    order_n = gram_mat.shape[0]
    identity = jnp.eye(order_n, dtype=gram_mat.dtype)
    thresh_sq = shrink_ratio * jnp.trace(gram_mat) / order_n
    shifted = gram_mat - thresh_sq * identity
    signum = shifted / jnp.sqrt(jnp.sum(shifted * shifted))

    def sign_step(turn_no, current):
        return 1.5 * current - 0.5 * matmul_hi(matmul_hi(current, current), current)

    signum = lax.fori_loop(0, SIGN_ITERS, sign_step, signum)
    keeper = 0.5 * (identity + signum)
    floored = 0.5 * (gram_mat + thresh_sq * identity + matmul_hi(shifted, signum))
    scale_c = jnp.sqrt(jnp.sum(floored * floored))

    def root_step(turn_no, state_pair):
        root_iter, inv_iter = state_pair
        step_mat = 0.5 * (3.0 * identity - matmul_hi(inv_iter, root_iter))
        return (matmul_hi(root_iter, step_mat), matmul_hi(step_mat, inv_iter))

    root_iter, inv_iter = lax.fori_loop(0, ROOT_ITERS, root_step, (floored / scale_c, identity))
    inv_root = inv_iter / jnp.sqrt(scale_c)
    return matmul_hi(keeper, identity - jnp.sqrt(thresh_sq) * inv_root)


def phase_of(index, period):
    angle = (2.0 * math.pi / period) * (index % period).astype(jnp.float32)
    return jnp.cos(angle), jnp.sin(angle)


def exchange_sum(value, axis):
    count = lax.axis_size(axis)
    rows = value.shape[0]
    pieces = value.reshape((count, rows // count) + value.shape[1:])
    mine = jnp.sum(lax.all_to_all(pieces, axis, 0, 0, tiled=True), axis=0)
    spread = jnp.broadcast_to(mine[None], pieces.shape)
    return lax.all_to_all(spread, axis, 0, 0, tiled=True).reshape(value.shape)


def exchange_gather(value, axis):
    count = lax.axis_size(axis)
    spread = jnp.broadcast_to(value[None], (count,) + value.shape)
    return lax.all_to_all(spread, axis, 0, 0, tiled=True)


def data_gradient(sky_b, grid_tiles, freq_block, vis_block, vis_all):
    blocks_n, chan_count, row_count, block = sky_b.shape
    width = blocks_n * block
    n_facet = vis_all.shape[0]
    all_rows = n_facet * vis_all.shape[3]
    vb_n = vis_all.shape[4]
    row0 = lax.axis_index("facet") * row_count

    p_idx = lax.broadcasted_iota(jnp.int32, (row_count, n_facet, vis_all.shape[3]), 1) * vis_all.shape[
        3
    ] + lax.broadcasted_iota(jnp.int32, (row_count, n_facet, vis_all.shape[3]), 2)
    q_idx = lax.broadcasted_iota(jnp.int32, (row_count, n_facet, vis_all.shape[3]), 0) + row0
    cos_c, sin_c = phase_of(p_idx * q_idx, all_rows)
    col_scale = 1.0 / math.sqrt(all_rows)
    v_re = vis_all[:, :, 0]
    v_im = vis_all[:, :, 1]
    u_re = (
        jnp.einsum("qfp,fcpvm->cvqm", cos_c, v_re, precision=HI)
        - jnp.einsum("qfp,fcpvm->cvqm", sin_c, v_im, precision=HI)
    ) * col_scale
    u_im = (
        jnp.einsum("qfp,fcpvm->cvqm", sin_c, v_re, precision=HI)
        + jnp.einsum("qfp,fcpvm->cvqm", cos_c, v_im, precision=HI)
    ) * col_scale

    n2_idx = lax.broadcasted_iota(jnp.int32, freq_block.shape + (blocks_n,), 2)
    w_cos, w_sin = phase_of(freq_block[:, :, None] * n2_idx, blocks_n)
    n1_idx = lax.broadcasted_iota(jnp.int32, freq_block.shape + (block,), 2)
    t_cos, t_sin = phase_of(freq_block[:, :, None] * n1_idx, width)
    t_cos = t_cos[:, :, None, :]
    t_sin = t_sin[:, :, None, :]
    j_idx = lax.broadcasted_iota(jnp.int32, (block, block), 0)
    m_idx = lax.broadcasted_iota(jnp.int32, (block, block), 1)
    f_cos, f_sin = phase_of(j_idx * m_idx, block)
    row_scale = 1.0 / math.sqrt(width)

    y_re = jnp.einsum("ctn,ncrm->ctrm", w_cos, sky_b, precision=HI)
    y_im = -jnp.einsum("ctn,ncrm->ctrm", w_sin, sky_b, precision=HI)
    yt_re = y_re * t_cos + y_im * t_sin
    yt_im = y_im * t_cos - y_re * t_sin
    tiles_n = freq_block.shape[1]
    flat = chan_count * tiles_n * row_count
    yt_re = yt_re.reshape(flat, block)
    yt_im = yt_im.reshape(flat, block)
    s_re = (matmul_hi(yt_re, f_cos) + matmul_hi(yt_im, f_sin)) * row_scale
    s_im = (matmul_hi(yt_im, f_cos) - matmul_hi(yt_re, f_sin)) * row_scale
    s_re = s_re.reshape(chan_count, tiles_n, row_count, block)
    s_im = s_im.reshape(chan_count, tiles_n, row_count, block)
    z_re = jnp.einsum("ctrj,ctjm->ctrm", s_re, grid_tiles, precision=HI)
    z_im = jnp.einsum("ctrj,ctjm->ctrm", s_im, grid_tiles, precision=HI)
    place = jax.nn.one_hot(vis_block, vb_n, dtype=jnp.float32)
    r_re = jnp.einsum("ctv,ctrm->cvrm", place, z_re, precision=HI) - u_re
    r_im = jnp.einsum("ctv,ctrm->cvrm", place, z_im, precision=HI) - u_im
    sp_re = jnp.einsum("ctv,cvrm->ctrm", place, r_re, precision=HI)
    sp_im = jnp.einsum("ctv,cvrm->ctrm", place, r_im, precision=HI)
    c_re = jnp.einsum("ctrm,ctjm->ctrj", sp_re, grid_tiles, precision=HI)
    c_im = jnp.einsum("ctrm,ctjm->ctrj", sp_im, grid_tiles, precision=HI)
    c_re = c_re.reshape(flat, block)
    c_im = c_im.reshape(flat, block)
    d_re = (matmul_hi(c_re, f_cos) - matmul_hi(c_im, f_sin)) * row_scale
    d_im = (matmul_hi(c_re, f_sin) + matmul_hi(c_im, f_cos)) * row_scale
    d_re = d_re.reshape(chan_count, tiles_n, row_count, block)
    d_im = d_im.reshape(chan_count, tiles_n, row_count, block)
    dt_re = d_re * t_cos - d_im * t_sin
    dt_im = d_im * t_cos + d_re * t_sin
    return jnp.einsum("ctn,ctrm->ncrm", w_cos, dt_re, precision=HI) - jnp.einsum(
        "ctn,ctrm->ncrm", w_sin, dt_im, precision=HI
    )


def on_device(sky_image, dual_field, sketch_matrix, grid_tiles, freq_block, vis_block, vis_data):
    chan_count, row_count, width = sky_image.shape
    block = grid_tiles.shape[2]
    blocks_n = width // block
    dual_b = lax.all_to_all(
        dual_field.reshape(blocks_n, chan_count, row_count, block), "chan", 0, 0, tiled=True
    )
    vis_all = exchange_gather(vis_data, "facet")
    sky_b = jnp.transpose(sky_image.reshape(chan_count, row_count, blocks_n, block), (2, 0, 1, 3))
    padded = padded_2(sky_b, (("facet", 2),), 1)
    grad_b = data_gradient(sky_b, grid_tiles, freq_block, vis_block, vis_all)
    smooth = 2.0 * sky_b - padded[:, :, :-2] - padded[:, :, 2:]
    new_b = sky_b - step_primal * (grad_b + smooth_weight * smooth + dual_b)
    new_image = jnp.transpose(new_b, (1, 2, 0, 3)).reshape(chan_count, row_count, width)
    rest = (1.0 - step_dual) * sky_b - 2.0 * step_dual * step_primal * (
        grad_b + smooth_weight * smooth
    )
    rest_pix = lax.all_to_all(rest, "chan", 0, 0, tiled=True).reshape(dual_field.shape)
    pixels = (1.0 - 2.0 * step_dual * step_primal) * dual_field + rest_pix
    chans = pixels.shape[0]
    flat_pix = pixels.reshape(chans, -1)
    sketch_rows = sketch_matrix.astype(jnp.float32).reshape(flat_pix.shape[1], -1)
    rank = sketch_rows.shape[1]
    part = jnp.concatenate(
        [matmul_hi(flat_pix, sketch_rows), jnp.dot(flat_pix, flat_pix.T, precision=HI)], axis=1
    )
    total = exchange_sum(part, "chan")
    sketch = total[:, :rank]
    outer = total[:, rank:]
    lower_fac = jnp.linalg.cholesky(matmul_hi(sketch.T, sketch))
    basis_mat = jax.scipy.linalg.solve_triangular(lower_fac, sketch.T, lower=True).T
    gram_mat = matmul_hi(basis_mat.T, matmul_hi(outer, basis_mat))
    shrink = shrink_matrix(gram_mat)
    coords = matmul_hi(basis_mat.T, flat_pix)
    new_dual = flat_pix - matmul_hi(matmul_hi(basis_mat, shrink), coords)
    return (new_image, new_dual.reshape(pixels.shape))


def solution(mesh):
    placed = (
        P("chan", "facet", None),
        P(None, "facet", "chan"),
        P("facet", "chan", None),
        P("chan", None, None, None),
        P("chan", None),
        P("chan", None),
        P("chan", None, "facet", None, None),
    )
    return jax.shard_map(
        on_device,
        mesh=mesh,
        in_specs=placed,
        out_specs=(P("chan", "facet", None), P(None, "facet", "chan")),
        check_vma=False,
    )
```

profile of v0, /device:TPU:1, one launch (start us, length us, event | category | flops | bytes accessed | tf_op | source)
XLA Modules:
  0.0 169.1 jit_solution(14845574068927179924)
XLA Ops:
  0.7 1.1 copy.107
  1.8 1.2 broadcast_in_dim.7
  3.0 9.1 %all-to-all-start = ((f32[8,8,2,4,4,128]{5,3,4,1,2,0:T(4,128)}), f32[8,8,2,4,4,128]{5,3,4,1,2,0:T(4,128)}, u32[]{:S(2)}, u32[]{:S(2)}) async-start(f32[8,8,2,4,4,128]{5,3,4,1,2,0:T(4,128)} %broadcast_in_dim.7), calls=%async_computation | async-start | bytes 2097152 | tf_op jit(solution)/shard_map/all_to_all | solution.py:79
  12.1 0.4 reshape.88
  12.5 0.7 fusion.199
  13.2 3.3 %collective-permute-start = (f32[32,8,1,128]{3,0,2,1:T(8,128)}, f32[32,8,1,128]{3,0,2,1:T(8,128)S(1)}, u32[]{:S(2)}, u32[]{:S(2)}) collective-permute-start(f32[32,8,1,128]{3,0,2,1:T(8,128)} %get-tuple-element.75), channel_id=1, source_target_pairs={{0,32},{32,64},{64,96},{96,128},{128,160},{160,192},{192,224},{1,3... | collective-permute-start | bytes 393224 | tf_op jit(solution)/shard_map/ppermute | solution.py:25
  16.6 1.3 collective-permute-start.1
  18.2 0.6 convolution_negate_fusion
  18.7 0.6 multiply_subtract_fusion.1
  19.3 0.5 fusion.76
  19.9 0.5 fusion.80
  20.4 0.5 fusion.8
  20.9 1.9 %fusion.207 = f32[8,4,4,128]{3,2,1,0:T(4,128)S(1)} fusion(f32[8,4,4,128]{3,2,1,0:T(4,128)S(1)} %bitcast.197, f32[8,4,128,128]{3,2,1,0:T(8,128)S(1)} %copy-done), kind=kOutput, calls=%fused_computation.241 | convolution fusion | flops 25165824 | bytes 2228224 | tf_op jit(solution)/shard_map/ctrj,ctjm->ctrm/dot_general | solution.py:131
  22.7 0.3 fusion.37
  23.1 0.5 fusion.9
  23.5 1.9 %fusion.206 = f32[8,4,4,128]{3,2,1,0:T(4,128)S(1)} fusion(f32[8,4,4,128]{3,2,1,0:T(4,128)S(1)} %bitcast.198, f32[8,4,128,128]{3,2,1,0:T(8,128)S(1)} %copy-done), kind=kOutput, calls=%fused_computation.240 | convolution fusion | flops 25165824 | bytes 2228224 | tf_op jit(solution)/shard_map/ctrj,ctjm->ctrm/dot_general | solution.py:130
  25.4 0.3 fusion.44
  25.7 15.7 %all-to-all-done = f32[8,8,2,4,4,128]{5,3,4,1,2,0:T(4,128)} async-done(((f32[8,8,2,4,4,128]{5,3,4,1,2,0:T(4,128)}), f32[8,8,2,4,4,128]{5,3,4,1,2,0:T(4,128)}, u32[]{:S(2)}, u32[]{:S(2)}) %all-to-all-start) | async-done | bytes 1048608 | tf_op jit(solution)/shard_map/all_to_all | solution.py:79
  41.4 7.7 %all-to-all-start.1 = ((f32[32,8,4,128]{3,2,1,0:T(4,128)}), f32[32,8,4,128]{3,2,1,0:T(4,128)S(1)}, u32[]{:S(2)}, u32[]{:S(2)}) async-start(f32[32,8,4,128]{3,2,1,0:T(4,128)} %bitcast.38), calls=%async_computation.1 | async-start | bytes 1048576 | tf_op jit(solution)/shard_map/all_to_all | solution.py:156
  49.1 1.3 fusion.198
  50.4 0.8 convolution_bitcast_fusion.3
  51.2 0.8 convolution_bitcast_fusion.5
  52.0 0.8 convolution_bitcast_fusion.4
  52.8 0.8 convolution_bitcast_fusion.6
  54.0 3.4 %fusion.32 = f32[8,4,4,128]{3,2,1,0:T(4,128)S(1)} fusion(f32[8,4,128,128]{3,2,1,0:T(8,128)S(1)} %copy-done, f32[8,4,4,128]{3,1,2,0:T(4,128)S(1)} %fusion.34), kind=kOutput, calls=%fused_computation.67 | convolution fusion | flops 25165824 | bytes 2228224 | tf_op jit(solution)/shard_map/ctrm,ctjm->ctrj/dot_general | solution.py:138
  57.7 3.4 %fusion.39 = f32[8,4,4,128]{3,2,1,0:T(4,128)S(1)} fusion(f32[8,4,128,128]{3,2,1,0:T(8,128)S(1)} %copy-done, f32[8,4,4,128]{3,1,2,0:T(4,128)S(1)} %fusion.41), kind=kOutput, calls=%fused_computation.75 | convolution fusion | flops 25165824 | bytes 2228224 | tf_op jit(solution)/shard_map/ctrm,ctjm->ctrj/dot_general | solution.py:137
  61.0 0.5 fusion.78
  61.5 0.5 fusion.7
  62.0 0.5 fusion.82
  62.4 0.5 fusion.6
  62.9 1.6 fusion.57
  64.5 3.1 %multiply_subtract_fusion = (f32[32,8,4,128]{3,0,2,1:T(8,128)S(1)}, f32[8,4,32,128]{3,2,1,0:T(8,128)}) fusion(f32[32,8,4,128]{3,0,2,1:T(8,128)S(1)} %bitcast.184, f32[32,8,1,128]{3,0,2,1:T(8,128)} %collective-permute-done.1, f32[32,8,1,128]{3,0,2,1:T(8,128)S(1)} %collective-permute-done, f32[32,8,4,128]{3,2,1,0:T(4,128)S(1)} %all-to-all-done.1, ...), kind=kOutput, calls=%fused_computation.43 | convolution fusion | flops 8189952 | bytes 3047552 | tf_op jit(solution)/shard_map/ctn,ctrm->ncrm/dot_general | solution.py:147
  67.5 0.3 copy.130
  67.9 18.6 %all_to_all.25 = f32[32,8,4,128]{3,2,1,0:T(4,128)S(1)} all-to-all(f32[32,8,4,128]{3,2,1,0:T(4,128)S(1)} %copy.130), channel_id=1, replica_groups=mesh['facet'=8,'chan'=32] {'chan'}, dimensions={0} | all-to-all | bytes 1048576 | tf_op jit(solution)/shard_map/all_to_all | solution.py:169
  86.5 1.9 %convolution_bitcast_fusion.1 = f32[256,256]{0,1:T(8,128)S(1)} fusion(f32[32,8,4,128]{3,2,1,0:T(4,128)S(1)} %all_to_all.25, f32[256,4,128]{2,1,0:T(4,128)} %param.12), kind=kOutput, calls=%fused_computation.10 | convolution fusion | flops 402915328 | bytes 1310720 | tf_op jit(solution)/shard_map/dot_general | solution.py:176
  88.4 1.5 convolution_bitcast_fusion.2
  90.1 13.8 %all_to_all.26 = f32[32,8,384]{2,1,0:T(8,128)S(1)} all-to-all(f32[32,8,384]{2,1,0:T(8,128)S(1)} %bitcast.188), channel_id=1, replica_groups=mesh['facet'=8,'chan'=32] {'chan'}, dimensions={0} | all-to-all | bytes 786432 | tf_op jit(solution)/shard_map/all_to_all | solution.py:71
  104.0 0.8 broadcast_in_dim.8
  104.7 3.8 %all-to-all-start.4 = ((f32[32,8,384]{2,1,0:T(8,128)}), f32[32,8,384]{2,1,0:T(8,128)S(1)}, u32[]{:S(2)}, u32[]{:S(2)}) async-start(f32[32,8,384]{2,1,0:T(8,128)} %broadcast_in_dim.8), calls=%async_computation.4 | async-start | bytes 786432 | tf_op jit(solution)/shard_map/all_to_all | solution.py:73
  108.6 2.0 %reshape.98 = f32[8,4,4096]{2,1,0:T(4,128)} reshape(f32[8,4,32,128]{3,2,1,0:T(8,128)} %get-tuple-element.72) | data formatting | bytes 1048576 | tf_op jit(solution)/shard_map/reshape | solution.py:165
  110.6 8.2 %all-to-all-done.4 = f32[32,8,384]{2,1,0:T(8,128)S(1)} async-done(((f32[32,8,384]{2,1,0:T(8,128)}), f32[32,8,384]{2,1,0:T(8,128)S(1)}, u32[]{:S(2)}, u32[]{:S(2)}) %all-to-all-start.4) | async-done | bytes 393248 | tf_op jit(solution)/shard_map/all_to_all | solution.py:73
  118.8 0.4 fusion.24
  119.3 11.7 %cholesky.22 = f32[128,128]{1,0:T(8,128)S(1)} custom-call(f32[128,128]{1,0:T(8,128)S(1)} %fusion.31), custom_call_target="Cholesky" | custom-call | tf_op jit(solution)/shard_map/jit(cholesky)/cholesky | solution.py:181
  131.1 0.6 compare_reduce_fusion
  131.7 0.7 fusion.26
  132.4 9.8 %custom-call.7 = f32[1,128,128]{1,2,0:T(8,128)S(1)} custom-call(f32[1,128,128]{2,1,0:T(8,128)S(1)} %fusion.26), custom_call_target="InvertDiagBlocksLowerTriangular" | custom-call | tf_op jit(solution)/shard_map/jit(_solve_triangular)/triangular_solve | solution.py:182
  142.2 0.3 fusion.22
  142.5 0.4 fusion.20
  142.9 0.9 select_reduce_fusion
  144.4 0.6 multiply_reduce_fusion.1
  145.8 5.4 %while.23 = (s32[]{:T(128)}, f32[128,128]{1,0:T(8,128)S(1)}, s32[]{:T(128)}) while((s32[]{:T(128)}, f32[128,128]{1,0:T(8,128)S(1)}, s32[]{:T(128)}) %tuple.50), condition=%wide.region_6.7_spmd, body=%wide.region_5.6_spmd.sunk | while | flops 50380800 | bytes 458797 | solution.py:47
  151.2 0.8 multiply_reduce_fusion
  152.9 11.4 %while.24 = (s32[]{:T(128)}, f32[128,128]{0,1:T(8,128)S(1)}, f32[128,128]{1,0:T(8,128)S(1)}, s32[]{:T(128)}) while((s32[]{:T(128)}, f32[128,128]{0,1:T(8,128)S(1)}, f32[128,128]{1,0:T(8,128)S(1)}, s32[]{:T(128)}) %tuple.53), condition=%wide.region_9.10_spmd.clone, body=%wide.region_8.9_spmd.clone.sunk | while | flops 75563008 | bytes 852021 | solution.py:57
  153.4 0.3 convolution_bitcast_fusion.8
  154.2 0.3 convolution_bitcast_fusion.8
  155.1 0.3 convolution_bitcast_fusion.8
  155.9 0.3 convolution_bitcast_fusion.8
  156.7 0.3 convolution_bitcast_fusion.8
  161.6 0.3 convolution_bitcast_fusion.8
  162.4 0.3 convolution_bitcast_fusion.8
  164.6 0.4 fusion.208
  165.0 1.5 fusion.10
  166.5 1.6 convolution_subtract_fusion.2
  168.1 1.0 reshape.103
  (134 shorter events, 15.6 us)
Async XLA Ops:
  0.6 20.2 %copy-start = (f32[8,4,128,128]{3,2,1,0:T(8,128)S(1)}, f32[8,4,128,128]{3,2,1,0:T(8,128)}, u32[]{:S(2)}) copy-start(f32[8,4,128,128]{3,2,1,0:T(8,128)} %param.14) | copy-start | bytes 6291460
  0.6 11.5 %copy-start.1 = (f32[8,4,4096]{2,1,0:T(4,128)S(1)}, f32[8,4,4096]{2,1,0:T(4,128)}, u32[]{:S(2)}) copy-start(f32[8,4,4096]{2,1,0:T(4,128)} %param.11) | copy-start | bytes 1572868
  3.0 14.9 %copy-start.3 = (s32[8,4]{0,1:T(4,128)S(1)}, s32[8,4]{0,1:T(4,128)}, u32[]{:S(2)}) copy-start(s32[8,4]{0,1:T(4,128)} %param.15) | copy-start | bytes 388
  3.0 38.4 %all-to-all-start = ((f32[8,8,2,4,4,128]{5,3,4,1,2,0:T(4,128)}), f32[8,8,2,4,4,128]{5,3,4,1,2,0:T(4,128)}, u32[]{:S(2)}, u32[]{:S(2)}) async-start(f32[8,8,2,4,4,128]{5,3,4,1,2,0:T(4,128)} %broadcast_in_dim.7), calls=%async_computation | async-start | bytes 2097152 | tf_op jit(solution)/shard_map/all_to_all | solution.py:79
  12.1 7.7 %copy-start.4 = (s32[8,4]{0,1:T(4,128)S(1)}, s32[8,4]{0,1:T(4,128)}, u32[]{:S(2)}) copy-start(s32[8,4]{0,1:T(4,128)} %param.16) | copy-start | bytes 388
  13.2 51.3 %collective-permute-start = (f32[32,8,1,128]{3,0,2,1:T(8,128)}, f32[32,8,1,128]{3,0,2,1:T(8,128)S(1)}, u32[]{:S(2)}, u32[]{:S(2)}) collective-permute-start(f32[32,8,1,128]{3,0,2,1:T(8,128)} %get-tuple-element.75), channel_id=1, source_target_pairs={{0,32},{32,64},{64,96},{96,128},{128,160},{160,192},{192,224},{1,3... | collective-permute-start | bytes 393224 | tf_op jit(solution)/shard_map/ppermute | solution.py:25
  16.6 47.9 %collective-permute-start.1 = (f32[32,8,1,128]{3,0,2,1:T(8,128)}, f32[32,8,1,128]{3,0,2,1:T(8,128)}, u32[]{:S(2)}, u32[]{:S(2)}) collective-permute-start(f32[32,8,1,128]{3,0,2,1:T(8,128)} %get-tuple-element.76), channel_id=1, source_target_pairs={{32,0},{64,32},{96,64},{128,96},{160,128},{192,160},{224,192},{33,... | collective-permute-start | bytes 393224 | tf_op jit(solution)/shard_map/ppermute | solution.py:28
  41.4 23.1 %all-to-all-start.1 = ((f32[32,8,4,128]{3,2,1,0:T(4,128)}), f32[32,8,4,128]{3,2,1,0:T(4,128)S(1)}, u32[]{:S(2)}, u32[]{:S(2)}) async-start(f32[32,8,4,128]{3,2,1,0:T(4,128)} %bitcast.38), calls=%async_computation.1 | async-start | bytes 1048576 | tf_op jit(solution)/shard_map/all_to_all | solution.py:156
  67.5 20.8 %copy-start.2 = (bf16[4,128,128]{2,1,0:T(8,128)(2,1)S(1)}, bf16[4,128,128]{2,1,0:T(8,128)(2,1)}, u32[]{:S(2)}) copy-start(bf16[4,128,128]{2,1,0:T(8,128)(2,1)} %param.13) | copy-start | bytes 393220
  104.7 14.1 %all-to-all-start.4 = ((f32[32,8,384]{2,1,0:T(8,128)}), f32[32,8,384]{2,1,0:T(8,128)S(1)}, u32[]{:S(2)}, u32[]{:S(2)}) async-start(f32[32,8,384]{2,1,0:T(8,128)} %broadcast_in_dim.8), calls=%async_computation.4 | async-start | bytes 786432 | tf_op jit(solution)/shard_map/all_to_all | solution.py:73
where the time goes:
time: 170 us; the launch traced here: 169 us
  matrix products  49.6 us (29%)
  blocking collectives  32.4 us (19%)
  starting transfers between devices  25.3 us (15%)
  other arithmetic  24 us (14%)
  waiting for transfers between devices  23.9 us (14%)
  local copies, waits for them, and re-layouts  9.6 us (6%)
  between operations  3.22 us (2%)
    dot_general x83, matrix products, matmul_hi(): return jnp.dot(first_mat, second_mat, precision=HI)  26.9 us
    all_to_all x1, blocking collectives, on_device(): lax.all_to_all(rest, 'chan', 0, 0, tiled=True).reshape(dual_field.shape)  18.6 us
    all_to_all x1, waiting for transfers between devices, exchange_gather(): return lax.all_to_all(spread, axis, 0, 0, tiled=True)  15.7 us
    all_to_all x1, blocking collectives, exchange_sum(): mine = jnp.sum(lax.all_to_all(pieces, axis, 0, 0, tiled=True), axis=0)  13.8 us
    another operation x3, other arithmetic, on_device(): lower_fac = jnp.linalg.cholesky(matmul_hi(sketch.T, sketch))  12.4 us
    another operation x2, other arithmetic, on_device(): jax.scipy.linalg.solve_triangular(lower_fac, sketch.T, lower=True)  10.5 us
    all_to_all x1, starting transfers between devices, exchange_gather(): return lax.all_to_all(spread, axis, 0, 0, tiled=True)  9.13 us
    all_to_all x1, waiting for transfers between devices, exchange_sum(): return lax.all_to_all(spread, axis, 0, 0, tiled=True).reshape(value.shape)  8.23 us
  transfers between devices with their start and end apart: 5, of which 2 were waited for; matrix products, arithmetic and copies ran while one was open for 15% of the time, Pallas kernels for 0%

commit v1 on v0

--- a/solution.py
+++ b/solution.py
@@ -4,6 +4,7 @@
 import jax.numpy as jnp
 from jax import lax
 from jax.sharding import PartitionSpec as P
+
 
 SIGN_ITERS = 12
 ROOT_ITERS = 14
@@ -54,7 +55,7 @@
         step_mat = 0.5 * (3.0 * identity - matmul_hi(inv_iter, root_iter))
         return (matmul_hi(root_iter, step_mat), matmul_hi(step_mat, inv_iter))
 
-    root_iter, inv_iter = lax.fori_loop(0, ROOT_ITERS, root_step, (floored / scale_c, identity))
+    _, inv_iter = lax.fori_loop(0, ROOT_ITERS, root_step, (floored / scale_c, identity))
     inv_root = inv_iter / jnp.sqrt(scale_c)
     return matmul_hi(keeper, identity - jnp.sqrt(thresh_sq) * inv_root)
 
@@ -149,7 +150,7 @@
     )
 
 
-def on_device(sky_image, dual_field, sketch_matrix, grid_tiles, freq_block, vis_block, vis_data):
+def _on_device(sky_image, dual_field, sketch_matrix, grid_tiles, freq_block, vis_block, vis_data):
     chan_count, row_count, width = sky_image.shape
     block = grid_tiles.shape[2]
     blocks_n = width // block
@@ -198,7 +199,7 @@
         P("chan", None, "facet", None, None),
     )
     return jax.shard_map(
-        on_device,
+        _on_device,
         mesh=mesh,
         in_specs=placed,
         out_specs=(P("chan", "facet", None), P(None, "facet", "chan")),

time: 170 us -> 170 us (level)
  no operation moved by 1% of the time
where the time goes in v1:
time: 170 us; the launch traced here: 169 us
  matrix products  49.6 us (29%)
  blocking collectives  32.4 us (19%)
  starting transfers between devices  25.3 us (15%)
  other arithmetic  24 us (14%)
  waiting for transfers between devices  23.9 us (14%)
  local copies, waits for them, and re-layouts  9.6 us (6%)
  between operations  3.22 us (2%)
    dot_general x83, matrix products, matmul_hi(): return jnp.dot(first_mat, second_mat, precision=HI)  26.9 us
    all_to_all x1, blocking collectives, _on_device(): lax.all_to_all(rest, 'chan', 0, 0, tiled=True).reshape(dual_field.shape)  18.6 us
    all_to_all x1, waiting for transfers between devices, exchange_gather(): return lax.all_to_all(spread, axis, 0, 0, tiled=True)  15.7 us
    all_to_all x1, blocking collectives, exchange_sum(): mine = jnp.sum(lax.all_to_all(pieces, axis, 0, 0, tiled=True), axis=0)  13.8 us
    another operation x3, other arithmetic, _on_device(): lower_fac = jnp.linalg.cholesky(matmul_hi(sketch.T, sketch))  12.4 us
    another operation x2, other arithmetic, _on_device(): jax.scipy.linalg.solve_triangular(lower_fac, sketch.T, lower=True)  10.5 us
    all_to_all x1, starting transfers between devices, exchange_gather(): return lax.all_to_all(spread, axis, 0, 0, tiled=True)  9.13 us
    all_to_all x1, waiting for transfers between devices, exchange_sum(): return lax.all_to_all(spread, axis, 0, 0, tiled=True).reshape(value.shape)  8.23 us
  transfers between devices with their start and end apart: 5, of which 2 were waited for; matrix products, arithmetic and copies ran while one was open for 15% of the time, Pallas kernels for 0%

profile of v1, /device:TPU:1, one launch (start us, length us, event | category | flops | bytes accessed | tf_op | source)
XLA Modules:
  0.0 169.1 jit_solution(14845574068927179924)
XLA Ops:
  0.7 1.1 copy.107
  1.8 1.2 broadcast_in_dim.7
  3.0 9.1 %all-to-all-start = ((f32[8,8,2,4,4,128]{5,3,4,1,2,0:T(4,128)}), f32[8,8,2,4,4,128]{5,3,4,1,2,0:T(4,128)}, u32[]{:S(2)}, u32[]{:S(2)}) async-start(f32[8,8,2,4,4,128]{5,3,4,1,2,0:T(4,128)} %broadcast_in_dim.7), calls=%async_computation | async-start | bytes 2097152 | tf_op jit(solution)/shard_map/all_to_all | solution.py:80
  12.1 0.4 reshape.88
  12.5 0.7 fusion.199
  13.2 3.3 %collective-permute-start = (f32[32,8,1,128]{3,0,2,1:T(8,128)}, f32[32,8,1,128]{3,0,2,1:T(8,128)S(1)}, u32[]{:S(2)}, u32[]{:S(2)}) collective-permute-start(f32[32,8,1,128]{3,0,2,1:T(8,128)} %get-tuple-element.75), channel_id=1, source_target_pairs={{0,32},{32,64},{64,96},{96,128},{128,160},{160,192},{192,224},{1,3... | collective-permute-start | bytes 393224 | tf_op jit(solution)/shard_map/ppermute | solution.py:26
  16.6 1.3 collective-permute-start.1
  18.2 0.6 convolution_negate_fusion
  18.7 0.6 multiply_subtract_fusion.1
  19.3 0.5 fusion.76
  19.9 0.5 fusion.80
  20.4 0.5 fusion.8
  20.9 1.9 %fusion.207 = f32[8,4,4,128]{3,2,1,0:T(4,128)S(1)} fusion(f32[8,4,4,128]{3,2,1,0:T(4,128)S(1)} %bitcast.197, f32[8,4,128,128]{3,2,1,0:T(8,128)S(1)} %copy-done), kind=kOutput, calls=%fused_computation.241 | convolution fusion | flops 25165824 | bytes 2228224 | tf_op jit(solution)/shard_map/ctrj,ctjm->ctrm/dot_general | solution.py:132
  22.7 0.3 fusion.37
  23.1 0.5 fusion.9
  23.5 1.9 %fusion.206 = f32[8,4,4,128]{3,2,1,0:T(4,128)S(1)} fusion(f32[8,4,4,128]{3,2,1,0:T(4,128)S(1)} %bitcast.198, f32[8,4,128,128]{3,2,1,0:T(8,128)S(1)} %copy-done), kind=kOutput, calls=%fused_computation.240 | convolution fusion | flops 25165824 | bytes 2228224 | tf_op jit(solution)/shard_map/ctrj,ctjm->ctrm/dot_general | solution.py:131
  25.4 0.3 fusion.44
  25.7 15.7 %all-to-all-done = f32[8,8,2,4,4,128]{5,3,4,1,2,0:T(4,128)} async-done(((f32[8,8,2,4,4,128]{5,3,4,1,2,0:T(4,128)}), f32[8,8,2,4,4,128]{5,3,4,1,2,0:T(4,128)}, u32[]{:S(2)}, u32[]{:S(2)}) %all-to-all-start) | async-done | bytes 1048608 | tf_op jit(solution)/shard_map/all_to_all | solution.py:80
  41.4 7.7 %all-to-all-start.1 = ((f32[32,8,4,128]{3,2,1,0:T(4,128)}), f32[32,8,4,128]{3,2,1,0:T(4,128)S(1)}, u32[]{:S(2)}, u32[]{:S(2)}) async-start(f32[32,8,4,128]{3,2,1,0:T(4,128)} %bitcast.38), calls=%async_computation.1 | async-start | bytes 1048576 | tf_op jit(solution)/shard_map/all_to_all | solution.py:157
  49.1 1.3 fusion.198
  50.4 0.8 convolution_bitcast_fusion.3
  51.2 0.8 convolution_bitcast_fusion.5
  52.0 0.8 convolution_bitcast_fusion.4
  52.8 0.8 convolution_bitcast_fusion.6
  54.0 3.4 %fusion.32 = f32[8,4,4,128]{3,2,1,0:T(4,128)S(1)} fusion(f32[8,4,128,128]{3,2,1,0:T(8,128)S(1)} %copy-done, f32[8,4,4,128]{3,1,2,0:T(4,128)S(1)} %fusion.34), kind=kOutput, calls=%fused_computation.67 | convolution fusion | flops 25165824 | bytes 2228224 | tf_op jit(solution)/shard_map/ctrm,ctjm->ctrj/dot_general | solution.py:139
  57.7 3.4 %fusion.39 = f32[8,4,4,128]{3,2,1,0:T(4,128)S(1)} fusion(f32[8,4,128,128]{3,2,1,0:T(8,128)S(1)} %copy-done, f32[8,4,4,128]{3,1,2,0:T(4,128)S(1)} %fusion.41), kind=kOutput, calls=%fused_computation.75 | convolution fusion | flops 25165824 | bytes 2228224 | tf_op jit(solution)/shard_map/ctrm,ctjm->ctrj/dot_general | solution.py:138
  61.0 0.5 fusion.78
  61.5 0.5 fusion.7
  62.0 0.5 fusion.82
  62.4 0.5 fusion.6
  62.9 1.6 fusion.57
  64.5 3.1 %multiply_subtract_fusion = (f32[32,8,4,128]{3,0,2,1:T(8,128)S(1)}, f32[8,4,32,128]{3,2,1,0:T(8,128)}) fusion(f32[32,8,4,128]{3,0,2,1:T(8,128)S(1)} %bitcast.184, f32[32,8,1,128]{3,0,2,1:T(8,128)} %collective-permute-done.1, f32[32,8,1,128]{3,0,2,1:T(8,128)S(1)} %collective-permute-done, f32[32,8,4,128]{3,2,1,0:T(4,128)S(1)} %all-to-all-done.1, ...), kind=kOutput, calls=%fused_computation.43 | convolution fusion | flops 8189952 | bytes 3047552 | tf_op jit(solution)/shard_map/ctn,ctrm->ncrm/dot_general | solution.py:148
  67.5 0.3 copy.130
  67.9 18.6 %all_to_all.25 = f32[32,8,4,128]{3,2,1,0:T(4,128)S(1)} all-to-all(f32[32,8,4,128]{3,2,1,0:T(4,128)S(1)} %copy.130), channel_id=1, replica_groups=mesh['facet'=8,'chan'=32] {'chan'}, dimensions={0} | all-to-all | bytes 1048576 | tf_op jit(solution)/shard_map/all_to_all | solution.py:170
  86.5 1.9 %convolution_bitcast_fusion.1 = f32[256,256]{0,1:T(8,128)S(1)} fusion(f32[32,8,4,128]{3,2,1,0:T(4,128)S(1)} %all_to_all.25, f32[256,4,128]{2,1,0:T(4,128)} %param.12), kind=kOutput, calls=%fused_computation.10 | convolution fusion | flops 402915328 | bytes 1310720 | tf_op jit(solution)/shard_map/dot_general | solution.py:177
  88.4 1.5 convolution_bitcast_fusion.2
  90.1 13.8 %all_to_all.26 = f32[32,8,384]{2,1,0:T(8,128)S(1)} all-to-all(f32[32,8,384]{2,1,0:T(8,128)S(1)} %bitcast.188), channel_id=1, replica_groups=mesh['facet'=8,'chan'=32] {'chan'}, dimensions={0} | all-to-all | bytes 786432 | tf_op jit(solution)/shard_map/all_to_all | solution.py:72
  104.0 0.8 broadcast_in_dim.8
  104.7 3.8 %all-to-all-start.4 = ((f32[32,8,384]{2,1,0:T(8,128)}), f32[32,8,384]{2,1,0:T(8,128)S(1)}, u32[]{:S(2)}, u32[]{:S(2)}) async-start(f32[32,8,384]{2,1,0:T(8,128)} %broadcast_in_dim.8), calls=%async_computation.4 | async-start | bytes 786432 | tf_op jit(solution)/shard_map/all_to_all | solution.py:74
  108.6 2.0 %reshape.98 = f32[8,4,4096]{2,1,0:T(4,128)} reshape(f32[8,4,32,128]{3,2,1,0:T(8,128)} %get-tuple-element.72) | data formatting | bytes 1048576 | tf_op jit(solution)/shard_map/reshape | solution.py:166
  110.6 8.2 %all-to-all-done.4 = f32[32,8,384]{2,1,0:T(8,128)S(1)} async-done(((f32[32,8,384]{2,1,0:T(8,128)}), f32[32,8,384]{2,1,0:T(8,128)S(1)}, u32[]{:S(2)}, u32[]{:S(2)}) %all-to-all-start.4) | async-done | bytes 393248 | tf_op jit(solution)/shard_map/all_to_all | solution.py:74
  118.8 0.4 fusion.24
  119.3 11.7 %cholesky.22 = f32[128,128]{1,0:T(8,128)S(1)} custom-call(f32[128,128]{1,0:T(8,128)S(1)} %fusion.31), custom_call_target="Cholesky" | custom-call | tf_op jit(solution)/shard_map/jit(cholesky)/cholesky | solution.py:182
  131.1 0.6 compare_reduce_fusion
  131.7 0.7 fusion.26
  132.4 9.8 %custom-call.7 = f32[1,128,128]{1,2,0:T(8,128)S(1)} custom-call(f32[1,128,128]{2,1,0:T(8,128)S(1)} %fusion.26), custom_call_target="InvertDiagBlocksLowerTriangular" | custom-call | tf_op jit(solution)/shard_map/jit(_solve_triangular)/triangular_solve | solution.py:183
  142.2 0.3 fusion.22
  142.5 0.4 fusion.20
  142.9 0.9 select_reduce_fusion
  144.4 0.6 multiply_reduce_fusion.1
  145.8 5.4 %while.23 = (s32[]{:T(128)}, f32[128,128]{1,0:T(8,128)S(1)}, s32[]{:T(128)}) while((s32[]{:T(128)}, f32[128,128]{1,0:T(8,128)S(1)}, s32[]{:T(128)}) %tuple.50), condition=%wide.region_6.7_spmd, body=%wide.region_5.6_spmd.sunk | while | flops 50380800 | bytes 458797 | solution.py:48
  151.2 0.8 multiply_reduce_fusion
  152.9 11.4 %while.24 = (s32[]{:T(128)}, f32[128,128]{0,1:T(8,128)S(1)}, f32[128,128]{1,0:T(8,128)S(1)}, s32[]{:T(128)}) while((s32[]{:T(128)}, f32[128,128]{0,1:T(8,128)S(1)}, f32[128,128]{1,0:T(8,128)S(1)}, s32[]{:T(128)}) %tuple.53), condition=%wide.region_9.10_spmd.clone, body=%wide.region_8.9_spmd.clone.sunk | while | flops 75563008 | bytes 852021 | solution.py:58
  153.4 0.3 convolution_bitcast_fusion.8
  154.2 0.3 convolution_bitcast_fusion.8
  155.1 0.3 convolution_bitcast_fusion.8
  155.9 0.3 convolution_bitcast_fusion.8
  156.7 0.3 convolution_bitcast_fusion.8
  157.5 0.3 convolution_bitcast_fusion.8
  164.0 0.3 convolution_bitcast_fusion.8
  164.6 0.4 fusion.208
  165.0 1.5 fusion.10
  166.5 1.6 convolution_subtract_fusion.2
  168.1 1.0 reshape.103
  (134 shorter events, 15.6 us)
Async XLA Ops:
  0.6 20.2 %copy-start = (f32[8,4,128,128]{3,2,1,0:T(8,128)S(1)}, f32[8,4,128,128]{3,2,1,0:T(8,128)}, u32[]{:S(2)}) copy-start(f32[8,4,128,128]{3,2,1,0:T(8,128)} %param.14) | copy-start | bytes 6291460
  0.6 11.5 %copy-start.1 = (f32[8,4,4096]{2,1,0:T(4,128)S(1)}, f32[8,4,4096]{2,1,0:T(4,128)}, u32[]{:S(2)}) copy-start(f32[8,4,4096]{2,1,0:T(4,128)} %param.11) | copy-start | bytes 1572868
  3.0 14.9 %copy-start.3 = (s32[8,4]{0,1:T(4,128)S(1)}, s32[8,4]{0,1:T(4,128)}, u32[]{:S(2)}) copy-start(s32[8,4]{0,1:T(4,128)} %param.15) | copy-start | bytes 388
  3.0 38.4 %all-to-all-start = ((f32[8,8,2,4,4,128]{5,3,4,1,2,0:T(4,128)}), f32[8,8,2,4,4,128]{5,3,4,1,2,0:T(4,128)}, u32[]{:S(2)}, u32[]{:S(2)}) async-start(f32[8,8,2,4,4,128]{5,3,4,1,2,0:T(4,128)} %broadcast_in_dim.7), calls=%async_computation | async-start | bytes 2097152 | tf_op jit(solution)/shard_map/all_to_all | solution.py:80
  12.1 7.7 %copy-start.4 = (s32[8,4]{0,1:T(4,128)S(1)}, s32[8,4]{0,1:T(4,128)}, u32[]{:S(2)}) copy-start(s32[8,4]{0,1:T(4,128)} %param.16) | copy-start | bytes 388
  13.2 51.3 %collective-permute-start = (f32[32,8,1,128]{3,0,2,1:T(8,128)}, f32[32,8,1,128]{3,0,2,1:T(8,128)S(1)}, u32[]{:S(2)}, u32[]{:S(2)}) collective-permute-start(f32[32,8,1,128]{3,0,2,1:T(8,128)} %get-tuple-element.75), channel_id=1, source_target_pairs={{0,32},{32,64},{64,96},{96,128},{128,160},{160,192},{192,224},{1,3... | collective-permute-start | bytes 393224 | tf_op jit(solution)/shard_map/ppermute | solution.py:26
  16.6 47.9 %collective-permute-start.1 = (f32[32,8,1,128]{3,0,2,1:T(8,128)}, f32[32,8,1,128]{3,0,2,1:T(8,128)}, u32[]{:S(2)}, u32[]{:S(2)}) collective-permute-start(f32[32,8,1,128]{3,0,2,1:T(8,128)} %get-tuple-element.76), channel_id=1, source_target_pairs={{32,0},{64,32},{96,64},{128,96},{160,128},{192,160},{224,192},{33,... | collective-permute-start | bytes 393224 | tf_op jit(solution)/shard_map/ppermute | solution.py:29
  41.4 23.1 %all-to-all-start.1 = ((f32[32,8,4,128]{3,2,1,0:T(4,128)}), f32[32,8,4,128]{3,2,1,0:T(4,128)S(1)}, u32[]{:S(2)}, u32[]{:S(2)}) async-start(f32[32,8,4,128]{3,2,1,0:T(4,128)} %bitcast.38), calls=%async_computation.1 | async-start | bytes 1048576 | tf_op jit(solution)/shard_map/all_to_all | solution.py:157
  67.5 20.8 %copy-start.2 = (bf16[4,128,128]{2,1,0:T(8,128)(2,1)S(1)}, bf16[4,128,128]{2,1,0:T(8,128)(2,1)}, u32[]{:S(2)}) copy-start(bf16[4,128,128]{2,1,0:T(8,128)(2,1)} %param.13) | copy-start | bytes 393220
  104.7 14.1 %all-to-all-start.4 = ((f32[32,8,384]{2,1,0:T(8,128)}), f32[32,8,384]{2,1,0:T(8,128)S(1)}, u32[]{:S(2)}, u32[]{:S(2)}) async-start(f32[32,8,384]{2,1,0:T(8,128)} %broadcast_in_dim.8), calls=%async_computation.4 | async-start | bytes 786432 | tf_op jit(solution)/shard_map/all_to_all | solution.py:74

commit v2 on v1

--- a/solution.py
+++ b/solution.py
@@ -50,12 +50,15 @@
     floored = 0.5 * (gram_mat + thresh_sq * identity + matmul_hi(shifted, signum))
     scale_c = jnp.sqrt(jnp.sum(floored * floored))
 
-    def root_step(turn_no, state_pair):
-        root_iter, inv_iter = state_pair
+    def root_step(turn_no, stacked):
+        root_iter, inv_iter = stacked[:order_n], stacked[order_n:]
         step_mat = 0.5 * (3.0 * identity - matmul_hi(inv_iter, root_iter))
-        return (matmul_hi(root_iter, step_mat), matmul_hi(step_mat, inv_iter))
-
-    _, inv_iter = lax.fori_loop(0, ROOT_ITERS, root_step, (floored / scale_c, identity))
+        return matmul_hi(stacked, step_mat)
+
+    stacked = lax.fori_loop(
+        0, ROOT_ITERS, root_step, jnp.concatenate([floored / scale_c, identity], axis=0)
+    )
+    inv_iter = stacked[order_n:]
     inv_root = inv_iter / jnp.sqrt(scale_c)
     return matmul_hi(keeper, identity - jnp.sqrt(thresh_sq) * inv_root)
 

time: 170 us -> 168 us (0.988)
  matrix products: 49.6 us -> 47.3 us
    dot_general x83 -> x69, matrix products: 26.9 us -> 24.6 us  [matmul_hi(): return jnp.dot(first_mat, second_mat, precision=HI)]
  transfers between devices with their start and end apart: 5 -> 5, of which waited for: 2 -> 2; matrix products, arithmetic and copies ran while one was open for 15% -> 16% of each run, Pallas kernels for 0% -> 0%
where the time goes in v2:
time: 168 us; the launch traced here: 167 us
  matrix products  47.3 us (28%)
  blocking collectives  32.4 us (19%)
  starting transfers between devices  25.3 us (15%)
  other arithmetic  24 us (14%)
  waiting for transfers between devices  23.9 us (14%)
  local copies, waits for them, and re-layouts  9.66 us (6%)
  between operations  3.23 us (2%)
    dot_general x69, matrix products, matmul_hi(): return jnp.dot(first_mat, second_mat, precision=HI)  24.6 us
    all_to_all x1, blocking collectives, _on_device(): lax.all_to_all(rest, 'chan', 0, 0, tiled=True).reshape(dual_field.shape)  18.6 us
    all_to_all x1, waiting for transfers between devices, exchange_gather(): return lax.all_to_all(spread, axis, 0, 0, tiled=True)  15.7 us
    all_to_all x1, blocking collectives, exchange_sum(): mine = jnp.sum(lax.all_to_all(pieces, axis, 0, 0, tiled=True), axis=0)  13.8 us
    another operation x3, other arithmetic, _on_device(): lower_fac = jnp.linalg.cholesky(matmul_hi(sketch.T, sketch))  12.4 us
    another operation x2, other arithmetic, _on_device(): jax.scipy.linalg.solve_triangular(lower_fac, sketch.T, lower=True)  10.5 us
    all_to_all x1, starting transfers between devices, exchange_gather(): return lax.all_to_all(spread, axis, 0, 0, tiled=True)  9.13 us
    all_to_all x1, waiting for transfers between devices, exchange_sum(): return lax.all_to_all(spread, axis, 0, 0, tiled=True).reshape(value.shape)  8.23 us
  transfers between devices with their start and end apart: 5, of which 2 were waited for; matrix products, arithmetic and copies ran while one was open for 16% of the time, Pallas kernels for 0%

profile of v2, /device:TPU:1, one launch (start us, length us, event | category | flops | bytes accessed | tf_op | source)
XLA Modules:
  0.0 166.8 jit_solution(13138529681654183618)
XLA Ops:
  0.7 1.1 copy.111
  1.8 1.2 broadcast_in_dim.7
  3.0 9.1 %all-to-all-start = ((f32[8,8,2,4,4,128]{5,3,4,1,2,0:T(4,128)}), f32[8,8,2,4,4,128]{5,3,4,1,2,0:T(4,128)}, u32[]{:S(2)}, u32[]{:S(2)}) async-start(f32[8,8,2,4,4,128]{5,3,4,1,2,0:T(4,128)} %broadcast_in_dim.7), calls=%async_computation | async-start | bytes 2097152 | tf_op jit(solution)/shard_map/all_to_all | solution.py:83
  12.1 0.4 reshape.88
  12.5 0.7 fusion.201
  13.2 3.3 %collective-permute-start = (f32[32,8,1,128]{3,0,2,1:T(8,128)}, f32[32,8,1,128]{3,0,2,1:T(8,128)S(1)}, u32[]{:S(2)}, u32[]{:S(2)}) collective-permute-start(f32[32,8,1,128]{3,0,2,1:T(8,128)} %get-tuple-element.61), channel_id=1, source_target_pairs={{0,32},{32,64},{64,96},{96,128},{128,160},{160,192},{192,224},{1,3... | collective-permute-start | bytes 393224 | tf_op jit(solution)/shard_map/ppermute | solution.py:26
  16.6 1.3 collective-permute-start.1
  18.2 0.6 convolution_negate_fusion
  18.7 0.6 multiply_subtract_fusion.1
  19.3 0.5 fusion.78
  19.9 0.5 fusion.82
  20.4 0.5 fusion.10
  20.9 1.9 %fusion.208 = f32[8,4,4,128]{3,2,1,0:T(4,128)S(1)} fusion(f32[8,4,4,128]{3,2,1,0:T(4,128)S(1)} %bitcast.185, f32[8,4,128,128]{3,2,1,0:T(8,128)S(1)} %copy-done), kind=kOutput, calls=%fused_computation.243 | convolution fusion | flops 25165824 | bytes 2228224 | tf_op jit(solution)/shard_map/ctrj,ctjm->ctrm/dot_general | solution.py:135
  22.7 0.3 fusion.43
  23.1 0.5 fusion.11
  23.5 1.9 %fusion.207 = f32[8,4,4,128]{3,2,1,0:T(4,128)S(1)} fusion(f32[8,4,4,128]{3,2,1,0:T(4,128)S(1)} %bitcast.186, f32[8,4,128,128]{3,2,1,0:T(8,128)S(1)} %copy-done), kind=kOutput, calls=%fused_computation.242 | convolution fusion | flops 25165824 | bytes 2228224 | tf_op jit(solution)/shard_map/ctrj,ctjm->ctrm/dot_general | solution.py:134
  25.4 0.3 fusion.50
  25.7 15.7 %all-to-all-done = f32[8,8,2,4,4,128]{5,3,4,1,2,0:T(4,128)} async-done(((f32[8,8,2,4,4,128]{5,3,4,1,2,0:T(4,128)}), f32[8,8,2,4,4,128]{5,3,4,1,2,0:T(4,128)}, u32[]{:S(2)}, u32[]{:S(2)}) %all-to-all-start) | async-done | bytes 1048608 | tf_op jit(solution)/shard_map/all_to_all | solution.py:83
  41.4 7.7 %all-to-all-start.1 = ((f32[32,8,4,128]{3,2,1,0:T(4,128)}), f32[32,8,4,128]{3,2,1,0:T(4,128)S(1)}, u32[]{:S(2)}, u32[]{:S(2)}) async-start(f32[32,8,4,128]{3,2,1,0:T(4,128)} %bitcast.38), calls=%async_computation.1 | async-start | bytes 1048576 | tf_op jit(solution)/shard_map/all_to_all | solution.py:160
  49.1 1.3 fusion.200
  50.4 0.8 convolution_bitcast_fusion.3
  51.2 0.8 convolution_bitcast_fusion.5
  52.0 0.8 convolution_bitcast_fusion.4
  52.8 0.8 convolution_bitcast_fusion.6
  54.0 3.4 %fusion.38 = f32[8,4,4,128]{3,2,1,0:T(4,128)S(1)} fusion(f32[8,4,128,128]{3,2,1,0:T(8,128)S(1)} %copy-done, f32[8,4,4,128]{3,1,2,0:T(4,128)S(1)} %fusion.40), kind=kOutput, calls=%fused_computation.74 | convolution fusion | flops 25165824 | bytes 2228224 | tf_op jit(solution)/shard_map/ctrm,ctjm->ctrj/dot_general | solution.py:142
  57.7 3.4 %fusion.45 = f32[8,4,4,128]{3,2,1,0:T(4,128)S(1)} fusion(f32[8,4,128,128]{3,2,1,0:T(8,128)S(1)} %copy-done, f32[8,4,4,128]{3,1,2,0:T(4,128)S(1)} %fusion.47), kind=kOutput, calls=%fused_computation.82 | convolution fusion | flops 25165824 | bytes 2228224 | tf_op jit(solution)/shard_map/ctrm,ctjm->ctrj/dot_general | solution.py:141
  61.0 0.5 fusion.80
  61.5 0.5 fusion.9
  62.0 0.5 fusion.84
  62.4 0.5 fusion.8
  62.9 1.6 fusion.59
  64.5 3.1 %multiply_subtract_fusion = (f32[32,8,4,128]{3,0,2,1:T(8,128)S(1)}, f32[8,4,32,128]{3,2,1,0:T(8,128)}) fusion(f32[32,8,4,128]{3,0,2,1:T(8,128)S(1)} %bitcast.172, f32[32,8,1,128]{3,0,2,1:T(8,128)} %collective-permute-done.1, f32[32,8,1,128]{3,0,2,1:T(8,128)S(1)} %collective-permute-done, f32[32,8,4,128]{3,2,1,0:T(4,128)S(1)} %all-to-all-done.1, ...), kind=kOutput, calls=%fused_computation.45 | convolution fusion | flops 8189952 | bytes 3047552 | tf_op jit(solution)/shard_map/ctn,ctrm->ncrm/dot_general | solution.py:151
  67.5 0.3 copy.134
  67.9 18.6 %all_to_all.25 = f32[32,8,4,128]{3,2,1,0:T(4,128)S(1)} all-to-all(f32[32,8,4,128]{3,2,1,0:T(4,128)S(1)} %copy.134), channel_id=1, replica_groups=mesh['facet'=8,'chan'=32] {'chan'}, dimensions={0} | all-to-all | bytes 1048576 | tf_op jit(solution)/shard_map/all_to_all | solution.py:173
  86.5 1.9 %convolution_bitcast_fusion.1 = f32[256,256]{0,1:T(8,128)S(1)} fusion(f32[32,8,4,128]{3,2,1,0:T(4,128)S(1)} %all_to_all.25, f32[256,4,128]{2,1,0:T(4,128)} %param.12), kind=kOutput, calls=%fused_computation.12 | convolution fusion | flops 402915328 | bytes 1310720 | tf_op jit(solution)/shard_map/dot_general | solution.py:180
  88.4 1.5 convolution_bitcast_fusion.2
  90.1 13.8 %all_to_all.26 = f32[32,8,384]{2,1,0:T(8,128)S(1)} all-to-all(f32[32,8,384]{2,1,0:T(8,128)S(1)} %bitcast.176), channel_id=1, replica_groups=mesh['facet'=8,'chan'=32] {'chan'}, dimensions={0} | all-to-all | bytes 786432 | tf_op jit(solution)/shard_map/all_to_all | solution.py:75
  104.0 0.8 broadcast_in_dim.8
  104.7 3.8 %all-to-all-start.4 = ((f32[32,8,384]{2,1,0:T(8,128)}), f32[32,8,384]{2,1,0:T(8,128)S(1)}, u32[]{:S(2)}, u32[]{:S(2)}) async-start(f32[32,8,384]{2,1,0:T(8,128)} %broadcast_in_dim.8), calls=%async_computation.4 | async-start | bytes 786432 | tf_op jit(solution)/shard_map/all_to_all | solution.py:77
  108.6 2.0 %reshape.98 = f32[8,4,4096]{2,1,0:T(4,128)} reshape(f32[8,4,32,128]{3,2,1,0:T(8,128)} %get-tuple-element.58) | data formatting | bytes 1048576 | tf_op jit(solution)/shard_map/reshape | solution.py:169
  110.6 8.2 %all-to-all-done.4 = f32[32,8,384]{2,1,0:T(8,128)S(1)} async-done(((f32[32,8,384]{2,1,0:T(8,128)}), f32[32,8,384]{2,1,0:T(8,128)S(1)}, u32[]{:S(2)}, u32[]{:S(2)}) %all-to-all-start.4) | async-done | bytes 393248 | tf_op jit(solution)/shard_map/all_to_all | solution.py:77
  118.8 0.4 fusion.26
  119.3 11.7 %cholesky.22 = f32[128,128]{1,0:T(8,128)S(1)} custom-call(f32[128,128]{1,0:T(8,128)S(1)} %fusion.37), custom_call_target="Cholesky" | custom-call | tf_op jit(solution)/shard_map/jit(cholesky)/cholesky | solution.py:185
  131.1 0.6 compare_reduce_fusion
  131.7 0.7 fusion.28
  132.4 9.8 %custom-call.7 = f32[1,128,128]{1,2,0:T(8,128)S(1)} custom-call(f32[1,128,128]{2,1,0:T(8,128)S(1)} %fusion.28), custom_call_target="InvertDiagBlocksLowerTriangular" | custom-call | tf_op jit(solution)/shard_map/jit(_solve_triangular)/triangular_solve | solution.py:186
  142.2 0.3 fusion.24
  142.5 0.4 fusion.22
  142.9 0.9 select_reduce_fusion
  144.4 0.6 multiply_reduce_fusion.1
  145.8 5.4 %while.21 = (s32[]{:T(128)}, f32[128,128]{1,0:T(8,128)S(1)}, s32[]{:T(128)}) while((s32[]{:T(128)}, f32[128,128]{1,0:T(8,128)S(1)}, s32[]{:T(128)}) %tuple.50), condition=%wide.region_6.7_spmd, body=%wide.region_5.6_spmd.sunk | while | flops 50380800 | bytes 458797 | solution.py:48
  151.2 0.8 multiply_reduce_fusion
  152.9 9.0 %while.22 = (s32[]{:T(128)}, f32[256,128]{0,1:T(8,128)S(1)}, s32[]{:T(128)}) while((s32[]{:T(128)}, f32[256,128]{0,1:T(8,128)S(1)}, s32[]{:T(128)}) %tuple.53), condition=%wide.region_9.10_spmd.clone, body=%wide.region_8.9_spmd.clone.sunk | while | flops 75563008 | bytes 786477 | solution.py:58
  153.2 0.3 convolution_bitcast_fusion.8
  155.8 0.3 convolution_bitcast_fusion.8
  156.5 0.3 convolution_bitcast_fusion.8
  157.7 0.3 convolution_bitcast_fusion.8
  158.4 0.3 convolution_bitcast_fusion.8
  159.7 0.3 convolution_bitcast_fusion.8
  160.3 0.3 convolution_bitcast_fusion.8
  162.2 0.4 fusion.209
  162.6 1.5 fusion.12
  164.2 1.6 convolution_subtract_fusion.2
  165.8 1.0 reshape.103
  (108 shorter events, 13.2 us)
Async XLA Ops:
  0.6 20.2 %copy-start = (f32[8,4,128,128]{3,2,1,0:T(8,128)S(1)}, f32[8,4,128,128]{3,2,1,0:T(8,128)}, u32[]{:S(2)}) copy-start(f32[8,4,128,128]{3,2,1,0:T(8,128)} %param.14) | copy-start | bytes 6291460
  0.6 11.5 %copy-start.1 = (f32[8,4,4096]{2,1,0:T(4,128)S(1)}, f32[8,4,4096]{2,1,0:T(4,128)}, u32[]{:S(2)}) copy-start(f32[8,4,4096]{2,1,0:T(4,128)} %param.11) | copy-start | bytes 1572868
  3.0 14.9 %copy-start.3 = (s32[8,4]{0,1:T(4,128)S(1)}, s32[8,4]{0,1:T(4,128)}, u32[]{:S(2)}) copy-start(s32[8,4]{0,1:T(4,128)} %param.15) | copy-start | bytes 388
  3.0 38.4 %all-to-all-start = ((f32[8,8,2,4,4,128]{5,3,4,1,2,0:T(4,128)}), f32[8,8,2,4,4,128]{5,3,4,1,2,0:T(4,128)}, u32[]{:S(2)}, u32[]{:S(2)}) async-start(f32[8,8,2,4,4,128]{5,3,4,1,2,0:T(4,128)} %broadcast_in_dim.7), calls=%async_computation | async-start | bytes 2097152 | tf_op jit(solution)/shard_map/all_to_all | solution.py:83
  12.1 7.7 %copy-start.4 = (s32[8,4]{0,1:T(4,128)S(1)}, s32[8,4]{0,1:T(4,128)}, u32[]{:S(2)}) copy-start(s32[8,4]{0,1:T(4,128)} %param.16) | copy-start | bytes 388
  13.2 51.3 %collective-permute-start = (f32[32,8,1,128]{3,0,2,1:T(8,128)}, f32[32,8,1,128]{3,0,2,1:T(8,128)S(1)}, u32[]{:S(2)}, u32[]{:S(2)}) collective-permute-start(f32[32,8,1,128]{3,0,2,1:T(8,128)} %get-tuple-element.61), channel_id=1, source_target_pairs={{0,32},{32,64},{64,96},{96,128},{128,160},{160,192},{192,224},{1,3... | collective-permute-start | bytes 393224 | tf_op jit(solution)/shard_map/ppermute | solution.py:26
  16.6 47.9 %collective-permute-start.1 = (f32[32,8,1,128]{3,0,2,1:T(8,128)}, f32[32,8,1,128]{3,0,2,1:T(8,128)}, u32[]{:S(2)}, u32[]{:S(2)}) collective-permute-start(f32[32,8,1,128]{3,0,2,1:T(8,128)} %get-tuple-element.62), channel_id=1, source_target_pairs={{32,0},{64,32},{96,64},{128,96},{160,128},{192,160},{224,192},{33,... | collective-permute-start | bytes 393224 | tf_op jit(solution)/shard_map/ppermute | solution.py:29
  41.4 23.1 %all-to-all-start.1 = ((f32[32,8,4,128]{3,2,1,0:T(4,128)}), f32[32,8,4,128]{3,2,1,0:T(4,128)S(1)}, u32[]{:S(2)}, u32[]{:S(2)}) async-start(f32[32,8,4,128]{3,2,1,0:T(4,128)} %bitcast.38), calls=%async_computation.1 | async-start | bytes 1048576 | tf_op jit(solution)/shard_map/all_to_all | solution.py:160
  67.5 20.8 %copy-start.2 = (bf16[4,128,128]{2,1,0:T(8,128)(2,1)S(1)}, bf16[4,128,128]{2,1,0:T(8,128)(2,1)}, u32[]{:S(2)}) copy-start(bf16[4,128,128]{2,1,0:T(8,128)(2,1)} %param.13) | copy-start | bytes 393220
  104.7 14.1 %all-to-all-start.4 = ((f32[32,8,384]{2,1,0:T(8,128)}), f32[32,8,384]{2,1,0:T(8,128)S(1)}, u32[]{:S(2)}, u32[]{:S(2)}) async-start(f32[32,8,384]{2,1,0:T(8,128)} %broadcast_in_dim.8), calls=%async_computation.4 | async-start | bytes 786432 | tf_op jit(solution)/shard_map/all_to_all | solution.py:77

commit v3 on v2

--- a/solution.py
+++ b/solution.py
@@ -4,6 +4,8 @@
 import jax.numpy as jnp
 from jax import lax
 from jax.sharding import PartitionSpec as P
+from jax.experimental import pallas as pl
+from jax.experimental.pallas import tpu as pltpu
 
 
 SIGN_ITERS = 12
@@ -61,6 +63,50 @@
     inv_iter = stacked[order_n:]
     inv_root = inv_iter / jnp.sqrt(scale_c)
     return matmul_hi(keeper, identity - jnp.sqrt(thresh_sq) * inv_root)
+
+
+def _basis_kernel(gram_ref, side_ref, out_ref, work_ref, rhs_ref):
+    order_n = gram_ref.shape[0]
+    work_ref[...] = gram_ref[...]
+    rhs_ref[...] = side_ref[...]
+    lanes = lax.broadcasted_iota(jnp.int32, (1, order_n), 1)
+    lanes_sq = lax.broadcasted_iota(jnp.int32, (order_n, order_n), 1)
+    subs = lax.broadcasted_iota(jnp.int32, (order_n, 1), 0)
+
+    def step(j, carry):
+        row = work_ref[pl.ds(j, 1), :]
+        pivot = jnp.sum(jnp.where(lanes == j, row, 0.0), axis=1, keepdims=True)
+        inv_diag = 1.0 / jnp.sqrt(pivot)
+        l_row = jnp.where(lanes >= j, row, 0.0) * inv_diag
+        solved = rhs_ref[pl.ds(j, 1), :] * inv_diag
+        out_ref[pl.ds(j, 1), :] = solved
+        work = work_ref[...]
+        col = jnp.sum(jnp.where(lanes_sq == j, work, 0.0), axis=1, keepdims=True)
+        l_col = jnp.where(subs >= j, col, 0.0) * inv_diag
+        work_ref[...] = work - l_col * l_row
+        rhs_ref[...] = rhs_ref[...] - l_col * solved
+        return carry
+
+    lax.fori_loop(0, order_n, step, 0)
+
+
+def basis_transposed(gram_mat, side):
+    order_n = gram_mat.shape[0]
+    return pl.pallas_call(
+        _basis_kernel,
+        out_shape=jax.ShapeDtypeStruct(side.shape, jnp.float32),
+        in_specs=[pl.BlockSpec(memory_space=pltpu.VMEM)] * 2,
+        out_specs=pl.BlockSpec(memory_space=pltpu.VMEM),
+        scratch_shapes=[
+            pltpu.VMEM(gram_mat.shape, jnp.float32),
+            pltpu.VMEM(side.shape, jnp.float32),
+        ],
+        cost_estimate=pl.CostEstimate(
+            flops=4 * order_n * order_n * (order_n + side.shape[1]),
+            transcendentals=order_n,
+            bytes_accessed=4 * (order_n * order_n + 2 * side.size),
+        ),
+    )(gram_mat, side)
 
 
 def phase_of(index, period):
@@ -182,8 +228,7 @@
     total = exchange_sum(part, "chan")
     sketch = total[:, :rank]
     outer = total[:, rank:]
-    lower_fac = jnp.linalg.cholesky(matmul_hi(sketch.T, sketch))
-    basis_mat = jax.scipy.linalg.solve_triangular(lower_fac, sketch.T, lower=True).T
+    basis_mat = basis_transposed(matmul_hi(sketch.T, sketch), sketch.T).T
     gram_mat = matmul_hi(basis_mat.T, matmul_hi(outer, basis_mat))
     shrink = shrink_matrix(gram_mat)
     coords = matmul_hi(basis_mat.T, flat_pix)

time: 168 us -> 165 us (0.982)
  other arithmetic: 24 us -> 1.71 us
  Pallas kernels: 0 us -> 16.1 us
  matrix products: 47.3 us -> 49.5 us
    another operation x5 -> x0, other arithmetic: 22.9 us -> none  [the longest x3 12.4 us: _on_device(): lower_fac = jnp.linalg.cholesky(matmul_hi(sketch.T, sketch))]
    pallas_call x0 -> x1, Pallas kernels: none -> 16.1 us  [basis_transposed(): pl.pallas_call(_basis_kernel, out_shape=jax.ShapeDtypeStruct(side.shape,...]
    dot_general x69, matrix products: 24.6 us -> 27.1 us  [matmul_hi(): return jnp.dot(first_mat, second_mat, precision=HI)]
where the time goes in v3:
time: 165 us; the launch traced here: 164 us
  matrix products  49.5 us (30%)
  blocking collectives  32.8 us (20%)
  starting transfers between devices  25.3 us (15%)
  waiting for transfers between devices  24.4 us (15%)
  Pallas kernels  16.1 us (10%)
  local copies, waits for them, and re-layouts  10 us (6%)
  between operations  3.21 us (2%)
  other arithmetic  1.71 us (1%)
    dot_general x69, matrix products, matmul_hi(): return jnp.dot(first_mat, second_mat, precision=HI)  27.1 us
    all_to_all x1, blocking collectives, _on_device(): lax.all_to_all(rest, 'chan', 0, 0, tiled=True).reshape(dual_field.shape)  18.6 us
    pallas_call x1, Pallas kernels, basis_transposed(): pl.pallas_call(_basis_kernel, out_shape=jax.ShapeDtypeStruct(side.shape,...  16.1 us
    all_to_all x1, waiting for transfers between devices, exchange_gather(): return lax.all_to_all(spread, axis, 0, 0, tiled=True)  15.7 us
    all_to_all x1, blocking collectives, exchange_sum(): mine = jnp.sum(lax.all_to_all(pieces, axis, 0, 0, tiled=True), axis=0)  14.2 us
    all_to_all x1, starting transfers between devices, exchange_gather(): return lax.all_to_all(spread, axis, 0, 0, tiled=True)  9.13 us
    all_to_all x1, waiting for transfers between devices, exchange_sum(): return lax.all_to_all(spread, axis, 0, 0, tiled=True).reshape(value.shape)  8.66 us
    all_to_all x1, starting transfers between devices, _on_device(): lax.all_to_all(dual_field.reshape(blocks_n, chan_count, row_count, block)...  7.69 us
  transfers between devices with their start and end apart: 5, of which 2 were waited for; matrix products, arithmetic and copies ran while one was open for 16% of the time, Pallas kernels for 0%

profile of v3, /device:TPU:1, one launch (start us, length us, event | category | flops | bytes accessed | tf_op | source)
XLA Modules:
  0.0 164.0 jit_solution(3242124965009401309)
XLA Ops:
  0.7 1.1 copy.110
  1.8 1.2 broadcast_in_dim.8
  3.0 9.1 %all-to-all-start = ((f32[8,8,2,4,4,128]{5,3,4,1,2,0:T(4,128)}), f32[8,8,2,4,4,128]{5,3,4,1,2,0:T(4,128)}, u32[]{:S(2)}, u32[]{:S(2)}) async-start(f32[8,8,2,4,4,128]{5,3,4,1,2,0:T(4,128)} %broadcast_in_dim.8), calls=%async_computation | async-start | bytes 2097152 | tf_op jit(solution)/shard_map/all_to_all | solution.py:129
  12.1 0.4 reshape.78
  12.5 0.7 fusion.196
  13.2 3.3 %collective-permute-start = (f32[32,8,1,128]{3,0,2,1:T(8,128)}, f32[32,8,1,128]{3,0,2,1:T(8,128)S(1)}, u32[]{:S(2)}, u32[]{:S(2)}) collective-permute-start(f32[32,8,1,128]{3,0,2,1:T(8,128)} %get-tuple-element.61), channel_id=1, source_target_pairs={{0,32},{32,64},{64,96},{96,128},{128,160},{160,192},{192,224},{1,3... | collective-permute-start | bytes 393224 | tf_op jit(solution)/shard_map/ppermute | solution.py:28
  16.5 1.3 collective-permute-start.1
  18.2 0.6 convolution_negate_fusion
  18.7 0.6 multiply_subtract_fusion.1
  19.3 0.5 fusion.71
  19.9 0.5 fusion.75
  20.4 0.5 fusion.10
  20.8 1.9 %fusion.203 = f32[8,4,4,128]{3,2,1,0:T(4,128)S(1)} fusion(f32[8,4,4,128]{3,2,1,0:T(4,128)S(1)} %bitcast.178, f32[8,4,128,128]{3,2,1,0:T(8,128)S(1)} %copy-done), kind=kOutput, calls=%fused_computation.233 | convolution fusion | flops 25165824 | bytes 2228224 | tf_op jit(solution)/shard_map/ctrj,ctjm->ctrm/dot_general | solution.py:181
  22.7 0.3 fusion.36
  23.0 0.5 fusion.11
  23.5 1.9 %fusion.202 = f32[8,4,4,128]{3,2,1,0:T(4,128)S(1)} fusion(f32[8,4,4,128]{3,2,1,0:T(4,128)S(1)} %bitcast.179, f32[8,4,128,128]{3,2,1,0:T(8,128)S(1)} %copy-done), kind=kOutput, calls=%fused_computation.232 | convolution fusion | flops 25165824 | bytes 2228224 | tf_op jit(solution)/shard_map/ctrj,ctjm->ctrm/dot_general | solution.py:180
  25.4 0.3 fusion.43
  25.7 15.7 %all-to-all-done = f32[8,8,2,4,4,128]{5,3,4,1,2,0:T(4,128)} async-done(((f32[8,8,2,4,4,128]{5,3,4,1,2,0:T(4,128)}), f32[8,8,2,4,4,128]{5,3,4,1,2,0:T(4,128)}, u32[]{:S(2)}, u32[]{:S(2)}) %all-to-all-start) | async-done | bytes 1048608 | tf_op jit(solution)/shard_map/all_to_all | solution.py:129
  41.4 7.7 %all-to-all-start.1 = ((f32[32,8,4,128]{3,2,1,0:T(4,128)}), f32[32,8,4,128]{3,2,1,0:T(4,128)S(1)}, u32[]{:S(2)}, u32[]{:S(2)}) async-start(f32[32,8,4,128]{3,2,1,0:T(4,128)} %bitcast.38), calls=%async_computation.1 | async-start | bytes 1048576 | tf_op jit(solution)/shard_map/all_to_all | solution.py:206
  49.1 1.3 fusion.195
  50.4 0.8 convolution_bitcast_fusion.3
  51.2 0.8 convolution_bitcast_fusion.5
  52.0 0.8 convolution_bitcast_fusion.4
  52.8 0.8 convolution_bitcast_fusion.6
  54.0 3.4 %fusion.31 = f32[8,4,4,128]{3,2,1,0:T(4,128)S(1)} fusion(f32[8,4,128,128]{3,2,1,0:T(8,128)S(1)} %copy-done, f32[8,4,4,128]{3,1,2,0:T(4,128)S(1)} %fusion.33), kind=kOutput, calls=%fused_computation.65 | convolution fusion | flops 25165824 | bytes 2228224 | tf_op jit(solution)/shard_map/ctrm,ctjm->ctrj/dot_general | solution.py:188
  57.7 3.4 %fusion.38 = f32[8,4,4,128]{3,2,1,0:T(4,128)S(1)} fusion(f32[8,4,128,128]{3,2,1,0:T(8,128)S(1)} %copy-done, f32[8,4,4,128]{3,1,2,0:T(4,128)S(1)} %fusion.40), kind=kOutput, calls=%fused_computation.73 | convolution fusion | flops 25165824 | bytes 2228224 | tf_op jit(solution)/shard_map/ctrm,ctjm->ctrj/dot_general | solution.py:187
  61.0 0.5 fusion.73
  61.5 0.5 fusion.9
  62.0 0.5 fusion.77
  62.4 0.5 fusion.8
  62.9 1.6 fusion.52
  64.5 3.1 %multiply_subtract_fusion = (f32[32,8,4,128]{3,0,2,1:T(8,128)S(1)}, f32[8,4,32,128]{3,2,1,0:T(8,128)}) fusion(f32[32,8,4,128]{3,0,2,1:T(8,128)S(1)} %bitcast.164, f32[32,8,1,128]{3,0,2,1:T(8,128)} %collective-permute-done.1, f32[32,8,1,128]{3,0,2,1:T(8,128)S(1)} %collective-permute-done, f32[32,8,4,128]{3,2,1,0:T(4,128)S(1)} %all-to-all-done.1, ...), kind=kOutput, calls=%fused_computation.45 | convolution fusion | flops 8189952 | bytes 3047552 | tf_op jit(solution)/shard_map/ctn,ctrm->ncrm/dot_general | solution.py:197
  67.5 0.3 copy.133
  67.9 18.6 %all_to_all.25 = f32[32,8,4,128]{3,2,1,0:T(4,128)S(1)} all-to-all(f32[32,8,4,128]{3,2,1,0:T(4,128)S(1)} %copy.133), channel_id=1, replica_groups=mesh['facet'=8,'chan'=32] {'chan'}, dimensions={0} | all-to-all | bytes 1048576 | tf_op jit(solution)/shard_map/all_to_all | solution.py:219
  86.5 1.9 %convolution_bitcast_fusion.1 = f32[256,256]{0,1:T(8,128)S(1)} fusion(f32[32,8,4,128]{3,2,1,0:T(4,128)S(1)} %all_to_all.25, f32[256,4,128]{2,1,0:T(4,128)} %param.12), kind=kOutput, calls=%fused_computation.12 | convolution fusion | flops 402915328 | bytes 1310720 | tf_op jit(solution)/shard_map/dot_general | solution.py:226
  88.4 1.5 convolution_bitcast_fusion.2
  90.0 0.9 copy.137
  90.9 14.2 %all_to_all.26 = f32[32,8,384]{2,1,0:T(8,128)S(1)} all-to-all(f32[32,8,384]{2,1,0:T(8,128)} %bitcast.168), channel_id=1, replica_groups=mesh['facet'=8,'chan'=32] {'chan'}, dimensions={0} | all-to-all | bytes 786432 | tf_op jit(solution)/shard_map/all_to_all | solution.py:121
  105.1 0.8 broadcast_in_dim.10
  105.9 3.8 %all-to-all-start.4 = ((f32[32,8,384]{2,1,0:T(8,128)}), f32[32,8,384]{2,1,0:T(8,128)S(1)}, u32[]{:S(2)}, u32[]{:S(2)}) async-start(f32[32,8,384]{2,1,0:T(8,128)} %broadcast_in_dim.10), calls=%async_computation.4 | async-start | bytes 786432 | tf_op jit(solution)/shard_map/all_to_all | solution.py:123
  109.7 0.6 fusion.47
  110.3 1.0 reshape.88
  111.3 8.7 %all-to-all-done.4 = f32[32,8,384]{2,1,0:T(8,128)S(1)} async-done(((f32[32,8,384]{2,1,0:T(8,128)}), f32[32,8,384]{2,1,0:T(8,128)S(1)}, u32[]{:S(2)}, u32[]{:S(2)}) %all-to-all-start.4) | async-done | bytes 393248 | tf_op jit(solution)/shard_map/all_to_all | solution.py:123
  120.0 1.0 fusion.188.gram_ref
  121.0 0.8 copy.160
  121.7 16.1 %shard_map.86 = f32[128,256]{1,0:T(8,128)} custom-call(f32[128,128]{1,0:T(8,128)} %fusion.188.gram_ref, f32[128,256]{1,0:T(8,128)} %bitcast.169), custom_call_target="tpu_custom_call" | custom-call | flops 25165824 | bytes 327680 | tf_op jit(solution)/shard_map/pallas_call | solution.py:95
  137.9 1.3 fusion.22
  139.2 1.8 %select_reduce_fusion = (f32[]{:T(128)}, f32[128,128]{1,0:T(8,128)S(1)}) fusion(f32[128,256]{1,0:T(8,128)} %shard_map.86, f32[256,128]{1,0:T(8,128)S(1)} %fusion.22), kind=kOutput, calls=%fused_computation.85 | convolution fusion | flops 50380800 | bytes 327684 | tf_op jit(solution)/shard_map/dot_general | solution.py:37
  141.7 0.6 multiply_reduce_fusion.1
  143.0 5.4 %while.21 = (s32[]{:T(128)}, f32[128,128]{1,0:T(8,128)S(1)}, s32[]{:T(128)}) while((s32[]{:T(128)}, f32[128,128]{1,0:T(8,128)S(1)}, s32[]{:T(128)}) %tuple.50), condition=%wide.region_4.5_spmd, body=%wide.region_3.4_spmd.sunk | while | flops 50380800 | bytes 458797 | solution.py:50
  148.4 0.8 multiply_reduce_fusion
  150.2 9.0 %while.22 = (s32[]{:T(128)}, f32[256,128]{0,1:T(8,128)S(1)}, s32[]{:T(128)}) while((s32[]{:T(128)}, f32[256,128]{0,1:T(8,128)S(1)}, s32[]{:T(128)}) %tuple.53), condition=%wide.region_7.8_spmd.clone, body=%wide.region_6.7_spmd.clone.sunk | while | flops 75563008 | bytes 786477 | solution.py:60
  151.1 0.3 convolution_bitcast_fusion.8
  151.8 0.3 convolution_bitcast_fusion.8
  153.1 0.3 convolution_bitcast_fusion.8
  153.7 0.3 convolution_bitcast_fusion.8
  155.0 0.3 convolution_bitcast_fusion.8
  155.6 0.3 convolution_bitcast_fusion.8
  156.9 0.3 convolution_bitcast_fusion.8
  157.6 0.3 convolution_bitcast_fusion.8
  159.5 0.4 fusion.204
  159.9 1.5 fusion.12
  161.4 1.7 %convolution_subtract_fusion.2 = f32[256,512]{1,0:T(8,128)S(1)} fusion(f32[256,128]{1,0:T(8,128)S(1)} %fusion.204, f32[128,512]{1,0:T(8,128)S(1)} %fusion.12, f32[32,8,4,128]{3,2,1,0:T(4,128)S(1)} %all_to_all.25, f32[256,4,128]{2,1,0:T(4,128)} %param.12), kind=kOutput, calls=%fused_computation.11 | convolution fusion | flops 201719808 | bytes 1966080 | tf_op jit(solution)/shard_map/dot_general | solution.py:37
  163.1 1.0 reshape.93
  (109 shorter events, 12.6 us)
Async XLA Ops:
  0.6 20.2 %copy-start = (f32[8,4,128,128]{3,2,1,0:T(8,128)S(1)}, f32[8,4,128,128]{3,2,1,0:T(8,128)}, u32[]{:S(2)}) copy-start(f32[8,4,128,128]{3,2,1,0:T(8,128)} %param.14) | copy-start | bytes 6291460
  0.6 11.5 %copy-start.3 = (f32[8,4,4096]{2,1,0:T(4,128)S(1)}, f32[8,4,4096]{2,1,0:T(4,128)}, u32[]{:S(2)}) copy-start(f32[8,4,4096]{2,1,0:T(4,128)} %param.11) | copy-start | bytes 1572868
  3.0 14.9 %copy-start.6 = (s32[8,4]{0,1:T(4,128)S(1)}, s32[8,4]{0,1:T(4,128)}, u32[]{:S(2)}) copy-start(s32[8,4]{0,1:T(4,128)} %param.15) | copy-start | bytes 388
  3.0 38.4 %all-to-all-start = ((f32[8,8,2,4,4,128]{5,3,4,1,2,0:T(4,128)}), f32[8,8,2,4,4,128]{5,3,4,1,2,0:T(4,128)}, u32[]{:S(2)}, u32[]{:S(2)}) async-start(f32[8,8,2,4,4,128]{5,3,4,1,2,0:T(4,128)} %broadcast_in_dim.8), calls=%async_computation | async-start | bytes 2097152 | tf_op jit(solution)/shard_map/all_to_all | solution.py:129
  12.1 7.7 %copy-start.7 = (s32[8,4]{0,1:T(4,128)S(1)}, s32[8,4]{0,1:T(4,128)}, u32[]{:S(2)}) copy-start(s32[8,4]{0,1:T(4,128)} %param.16) | copy-start | bytes 388
  13.2 51.3 %collective-permute-start = (f32[32,8,1,128]{3,0,2,1:T(8,128)}, f32[32,8,1,128]{3,0,2,1:T(8,128)S(1)}, u32[]{:S(2)}, u32[]{:S(2)}) collective-permute-start(f32[32,8,1,128]{3,0,2,1:T(8,128)} %get-tuple-element.61), channel_id=1, source_target_pairs={{0,32},{32,64},{64,96},{96,128},{128,160},{160,192},{192,224},{1,3... | collective-permute-start | bytes 393224 | tf_op jit(solution)/shard_map/ppermute | solution.py:28
  16.5 47.9 %collective-permute-start.1 = (f32[32,8,1,128]{3,0,2,1:T(8,128)}, f32[32,8,1,128]{3,0,2,1:T(8,128)}, u32[]{:S(2)}, u32[]{:S(2)}) collective-permute-start(f32[32,8,1,128]{3,0,2,1:T(8,128)} %get-tuple-element.62), channel_id=1, source_target_pairs={{32,0},{64,32},{96,64},{128,96},{160,128},{192,160},{224,192},{33,... | collective-permute-start | bytes 393224 | tf_op jit(solution)/shard_map/ppermute | solution.py:31
  41.4 23.1 %all-to-all-start.1 = ((f32[32,8,4,128]{3,2,1,0:T(4,128)}), f32[32,8,4,128]{3,2,1,0:T(4,128)S(1)}, u32[]{:S(2)}, u32[]{:S(2)}) async-start(f32[32,8,4,128]{3,2,1,0:T(4,128)} %bitcast.38), calls=%async_computation.1 | async-start | bytes 1048576 | tf_op jit(solution)/shard_map/all_to_all | solution.py:206
  67.5 20.8 %copy-start.5 = (bf16[4,128,128]{2,1,0:T(8,128)(2,1)S(1)}, bf16[4,128,128]{2,1,0:T(8,128)(2,1)}, u32[]{:S(2)}) copy-start(bf16[4,128,128]{2,1,0:T(8,128)(2,1)} %param.13) | copy-start | bytes 393220
  89.9 20.4 %copy-start.2 = (f32[8,4,32,128]{3,2,1,0:T(8,128)S(1)}, f32[8,4,32,128]{3,2,1,0:T(8,128)}, u32[]{:S(2)}) copy-start(f32[8,4,32,128]{3,2,1,0:T(8,128)} %get-tuple-element.58) | copy-start | bytes 1572868
  105.9 14.1 %all-to-all-start.4 = ((f32[32,8,384]{2,1,0:T(8,128)}), f32[32,8,384]{2,1,0:T(8,128)S(1)}, u32[]{:S(2)}, u32[]{:S(2)}) async-start(f32[32,8,384]{2,1,0:T(8,128)} %broadcast_in_dim.10), calls=%async_computation.4 | async-start | bytes 786432 | tf_op jit(solution)/shard_map/all_to_all | solution.py:123
  137.9 12.2 %copy-start.4 = (f32[128,128]{1,0:T(8,128)S(1)}, f32[128,128]{1,0:T(8,128)}, u32[]{:S(2)}) copy-start(f32[128,128]{1,0:T(8,128)} %fusion.47) | copy-start | bytes 196612
  150.1 9.3 %copy-start.1 = (f32[128,256]{1,0:T(8,128)S(1)}, f32[128,256]{1,0:T(8,128)}, u32[]{:S(2)}) copy-start(f32[128,256]{1,0:T(8,128)} %shard_map.86) | copy-start | bytes 393220

commit v4 on v3

--- a/solution.py
+++ b/solution.py
@@ -73,21 +73,32 @@
     lanes_sq = lax.broadcasted_iota(jnp.int32, (order_n, order_n), 1)
     subs = lax.broadcasted_iota(jnp.int32, (order_n, 1), 0)
 
-    def step(j, carry):
-        row = work_ref[pl.ds(j, 1), :]
-        pivot = jnp.sum(jnp.where(lanes == j, row, 0.0), axis=1, keepdims=True)
-        inv_diag = 1.0 / jnp.sqrt(pivot)
-        l_row = jnp.where(lanes >= j, row, 0.0) * inv_diag
-        solved = rhs_ref[pl.ds(j, 1), :] * inv_diag
-        out_ref[pl.ds(j, 1), :] = solved
+    def pick(vec, k):
+        return jnp.sum(jnp.where(lanes == k, vec, 0.0), axis=1, keepdims=True)
+
+    def step(t, carry):
+        j = 2 * t
+        row0 = work_ref[pl.ds(j, 1), :]
+        row1 = work_ref[pl.ds(j + 1, 1), :]
+        diag0 = jnp.sqrt(pick(row0, j))
+        low10 = pick(row0, j + 1) / diag0
+        diag1 = jnp.sqrt(pick(row1, j + 1) - low10 * low10)
+        l_row0 = jnp.where(lanes >= j, row0, 0.0) / diag0
+        l_row1 = jnp.where(lanes >= j + 1, row1 - l_row0 * low10, 0.0) / diag1
         work = work_ref[...]
-        col = jnp.sum(jnp.where(lanes_sq == j, work, 0.0), axis=1, keepdims=True)
-        l_col = jnp.where(subs >= j, col, 0.0) * inv_diag
-        work_ref[...] = work - l_col * l_row
-        rhs_ref[...] = rhs_ref[...] - l_col * solved
+        col0 = jnp.sum(jnp.where(lanes_sq == j, work, 0.0), axis=1, keepdims=True)
+        col1 = jnp.sum(jnp.where(lanes_sq == j + 1, work, 0.0), axis=1, keepdims=True)
+        l_col0 = jnp.where(subs >= j, col0, 0.0) / diag0
+        l_col1 = jnp.where(subs >= j + 1, col1 - l_col0 * low10, 0.0) / diag1
+        solved0 = rhs_ref[pl.ds(j, 1), :] / diag0
+        solved1 = (rhs_ref[pl.ds(j + 1, 1), :] - low10 * solved0) / diag1
+        out_ref[pl.ds(j, 1), :] = solved0
+        out_ref[pl.ds(j + 1, 1), :] = solved1
+        work_ref[...] = work - l_col0 * l_row0 - l_col1 * l_row1
+        rhs_ref[...] = rhs_ref[...] - l_col0 * solved0 - l_col1 * solved1
         return carry
 
-    lax.fori_loop(0, order_n, step, 0)
+    lax.fori_loop(0, order_n // 2, step, 0)
 
 
 def basis_transposed(gram_mat, side):

time: 165 us -> 159 us (0.964)
  Pallas kernels: 16.1 us -> 10.8 us
    pallas_call x1, Pallas kernels: 16.1 us -> 10.8 us  [basis_transposed(): pl.pallas_call(_basis_kernel, out_shape=jax.ShapeDtypeStruct(side.shape,...]
where the time goes in v4:
time: 159 us
  matrix products  49.5 us (31%)
  blocking collectives  32.8 us (21%)
  starting transfers between devices  25.3 us (16%)
  waiting for transfers between devices  24.4 us (15%)
  Pallas kernels  10.8 us (7%)
  local copies, waits for them, and re-layouts  10 us (6%)
  between operations  3.21 us (2%)
  other arithmetic  1.71 us (1%)
    dot_general x69, matrix products, matmul_hi(): return jnp.dot(first_mat, second_mat, precision=HI)  27.1 us
    all_to_all x1, blocking collectives, _on_device(): lax.all_to_all(rest, 'chan', 0, 0, tiled=True).reshape(dual_field.shape)  18.6 us
    all_to_all x1, waiting for transfers between devices, exchange_gather(): return lax.all_to_all(spread, axis, 0, 0, tiled=True)  15.7 us
    all_to_all x1, blocking collectives, exchange_sum(): mine = jnp.sum(lax.all_to_all(pieces, axis, 0, 0, tiled=True), axis=0)  14.2 us
    pallas_call x1, Pallas kernels, basis_transposed(): pl.pallas_call(_basis_kernel, out_shape=jax.ShapeDtypeStruct(side.shape,...  10.8 us
    all_to_all x1, starting transfers between devices, exchange_gather(): return lax.all_to_all(spread, axis, 0, 0, tiled=True)  9.13 us
    all_to_all x1, waiting for transfers between devices, exchange_sum(): return lax.all_to_all(spread, axis, 0, 0, tiled=True).reshape(value.shape)  8.66 us
    all_to_all x1, starting transfers between devices, _on_device(): lax.all_to_all(dual_field.reshape(blocks_n, chan_count, row_count, block)...  7.69 us
  transfers between devices with their start and end apart: 5, of which 2 were waited for; matrix products, arithmetic and copies ran while one was open for 16% of the time, Pallas kernels for 0%

profile of v4, /device:TPU:1, one launch (start us, length us, event | category | flops | bytes accessed | tf_op | source)
XLA Modules:
  0.0 158.7 jit_solution(3767112640441216837)
XLA Ops:
  0.7 1.1 copy.110
  1.8 1.2 broadcast_in_dim.8
  3.0 9.1 %all-to-all-start = ((f32[8,8,2,4,4,128]{5,3,4,1,2,0:T(4,128)}), f32[8,8,2,4,4,128]{5,3,4,1,2,0:T(4,128)}, u32[]{:S(2)}, u32[]{:S(2)}) async-start(f32[8,8,2,4,4,128]{5,3,4,1,2,0:T(4,128)} %broadcast_in_dim.8), calls=%async_computation | async-start | bytes 2097152 | tf_op jit(solution)/shard_map/all_to_all | solution.py:140
  12.1 0.4 reshape.78
  12.5 0.7 fusion.196
  13.2 3.3 %collective-permute-start = (f32[32,8,1,128]{3,0,2,1:T(8,128)}, f32[32,8,1,128]{3,0,2,1:T(8,128)S(1)}, u32[]{:S(2)}, u32[]{:S(2)}) collective-permute-start(f32[32,8,1,128]{3,0,2,1:T(8,128)} %get-tuple-element.61), channel_id=1, source_target_pairs={{0,32},{32,64},{64,96},{96,128},{128,160},{160,192},{192,224},{1,3... | collective-permute-start | bytes 393224 | tf_op jit(solution)/shard_map/ppermute | solution.py:28
  16.5 1.3 collective-permute-start.1
  18.2 0.6 convolution_negate_fusion
  18.7 0.6 multiply_subtract_fusion.1
  19.3 0.5 fusion.71
  19.9 0.5 fusion.75
  20.4 0.5 fusion.10
  20.8 1.9 %fusion.203 = f32[8,4,4,128]{3,2,1,0:T(4,128)S(1)} fusion(f32[8,4,4,128]{3,2,1,0:T(4,128)S(1)} %bitcast.178, f32[8,4,128,128]{3,2,1,0:T(8,128)S(1)} %copy-done), kind=kOutput, calls=%fused_computation.233 | convolution fusion | flops 25165824 | bytes 2228224 | tf_op jit(solution)/shard_map/ctrj,ctjm->ctrm/dot_general | solution.py:192
  22.7 0.3 fusion.36
  23.0 0.5 fusion.11
  23.5 1.9 %fusion.202 = f32[8,4,4,128]{3,2,1,0:T(4,128)S(1)} fusion(f32[8,4,4,128]{3,2,1,0:T(4,128)S(1)} %bitcast.179, f32[8,4,128,128]{3,2,1,0:T(8,128)S(1)} %copy-done), kind=kOutput, calls=%fused_computation.232 | convolution fusion | flops 25165824 | bytes 2228224 | tf_op jit(solution)/shard_map/ctrj,ctjm->ctrm/dot_general | solution.py:191
  25.4 0.3 fusion.43
  25.7 15.7 %all-to-all-done = f32[8,8,2,4,4,128]{5,3,4,1,2,0:T(4,128)} async-done(((f32[8,8,2,4,4,128]{5,3,4,1,2,0:T(4,128)}), f32[8,8,2,4,4,128]{5,3,4,1,2,0:T(4,128)}, u32[]{:S(2)}, u32[]{:S(2)}) %all-to-all-start) | async-done | bytes 1048608 | tf_op jit(solution)/shard_map/all_to_all | solution.py:140
  41.4 7.7 %all-to-all-start.1 = ((f32[32,8,4,128]{3,2,1,0:T(4,128)}), f32[32,8,4,128]{3,2,1,0:T(4,128)S(1)}, u32[]{:S(2)}, u32[]{:S(2)}) async-start(f32[32,8,4,128]{3,2,1,0:T(4,128)} %bitcast.38), calls=%async_computation.1 | async-start | bytes 1048576 | tf_op jit(solution)/shard_map/all_to_all | solution.py:217
  49.1 1.3 fusion.195
  50.4 0.8 convolution_bitcast_fusion.3
  51.2 0.8 convolution_bitcast_fusion.5
  52.0 0.8 convolution_bitcast_fusion.4
  52.8 0.8 convolution_bitcast_fusion.6
  54.0 3.4 %fusion.31 = f32[8,4,4,128]{3,2,1,0:T(4,128)S(1)} fusion(f32[8,4,128,128]{3,2,1,0:T(8,128)S(1)} %copy-done, f32[8,4,4,128]{3,1,2,0:T(4,128)S(1)} %fusion.33), kind=kOutput, calls=%fused_computation.65 | convolution fusion | flops 25165824 | bytes 2228224 | tf_op jit(solution)/shard_map/ctrm,ctjm->ctrj/dot_general | solution.py:199
  57.7 3.4 %fusion.38 = f32[8,4,4,128]{3,2,1,0:T(4,128)S(1)} fusion(f32[8,4,128,128]{3,2,1,0:T(8,128)S(1)} %copy-done, f32[8,4,4,128]{3,1,2,0:T(4,128)S(1)} %fusion.40), kind=kOutput, calls=%fused_computation.73 | convolution fusion | flops 25165824 | bytes 2228224 | tf_op jit(solution)/shard_map/ctrm,ctjm->ctrj/dot_general | solution.py:198
  61.0 0.5 fusion.73
  61.5 0.5 fusion.9
  62.0 0.5 fusion.77
  62.4 0.5 fusion.8
  62.9 1.6 fusion.52
  64.5 3.1 %multiply_subtract_fusion = (f32[32,8,4,128]{3,0,2,1:T(8,128)S(1)}, f32[8,4,32,128]{3,2,1,0:T(8,128)}) fusion(f32[32,8,4,128]{3,0,2,1:T(8,128)S(1)} %bitcast.164, f32[32,8,1,128]{3,0,2,1:T(8,128)} %collective-permute-done.1, f32[32,8,1,128]{3,0,2,1:T(8,128)S(1)} %collective-permute-done, f32[32,8,4,128]{3,2,1,0:T(4,128)S(1)} %all-to-all-done.1, ...), kind=kOutput, calls=%fused_computation.45 | convolution fusion | flops 8189952 | bytes 3047552 | tf_op jit(solution)/shard_map/ctn,ctrm->ncrm/dot_general | solution.py:208
  67.5 0.3 copy.133
  67.9 18.6 %all_to_all.25 = f32[32,8,4,128]{3,2,1,0:T(4,128)S(1)} all-to-all(f32[32,8,4,128]{3,2,1,0:T(4,128)S(1)} %copy.133), channel_id=1, replica_groups=mesh['facet'=8,'chan'=32] {'chan'}, dimensions={0} | all-to-all | bytes 1048576 | tf_op jit(solution)/shard_map/all_to_all | solution.py:230
  86.5 1.9 %convolution_bitcast_fusion.1 = f32[256,256]{0,1:T(8,128)S(1)} fusion(f32[32,8,4,128]{3,2,1,0:T(4,128)S(1)} %all_to_all.25, f32[256,4,128]{2,1,0:T(4,128)} %param.12), kind=kOutput, calls=%fused_computation.12 | convolution fusion | flops 402915328 | bytes 1310720 | tf_op jit(solution)/shard_map/dot_general | solution.py:237
  88.4 1.5 convolution_bitcast_fusion.2
  90.0 0.9 copy.137
  90.9 14.2 %all_to_all.26 = f32[32,8,384]{2,1,0:T(8,128)S(1)} all-to-all(f32[32,8,384]{2,1,0:T(8,128)} %bitcast.168), channel_id=1, replica_groups=mesh['facet'=8,'chan'=32] {'chan'}, dimensions={0} | all-to-all | bytes 786432 | tf_op jit(solution)/shard_map/all_to_all | solution.py:132
  105.1 0.8 broadcast_in_dim.10
  105.9 3.8 %all-to-all-start.4 = ((f32[32,8,384]{2,1,0:T(8,128)}), f32[32,8,384]{2,1,0:T(8,128)S(1)}, u32[]{:S(2)}, u32[]{:S(2)}) async-start(f32[32,8,384]{2,1,0:T(8,128)} %broadcast_in_dim.10), calls=%async_computation.4 | async-start | bytes 786432 | tf_op jit(solution)/shard_map/all_to_all | solution.py:134
  109.7 0.6 fusion.47
  110.3 1.0 reshape.88
  111.3 8.7 %all-to-all-done.4 = f32[32,8,384]{2,1,0:T(8,128)S(1)} async-done(((f32[32,8,384]{2,1,0:T(8,128)}), f32[32,8,384]{2,1,0:T(8,128)S(1)}, u32[]{:S(2)}, u32[]{:S(2)}) %all-to-all-start.4) | async-done | bytes 393248 | tf_op jit(solution)/shard_map/all_to_all | solution.py:134
  120.0 1.0 fusion.188.gram_ref
  121.0 0.8 copy.160
  121.7 10.8 %shard_map.86 = f32[128,256]{1,0:T(8,128)} custom-call(f32[128,128]{1,0:T(8,128)} %fusion.188.gram_ref, f32[128,256]{1,0:T(8,128)} %bitcast.169), custom_call_target="tpu_custom_call" | custom-call | flops 25165824 | bytes 327680 | tf_op jit(solution)/shard_map/pallas_call | solution.py:106
  132.5 1.3 fusion.22
  133.8 1.8 %select_reduce_fusion = (f32[]{:T(128)}, f32[128,128]{1,0:T(8,128)S(1)}) fusion(f32[128,256]{1,0:T(8,128)} %shard_map.86, f32[256,128]{1,0:T(8,128)S(1)} %fusion.22), kind=kOutput, calls=%fused_computation.85 | convolution fusion | flops 50380800 | bytes 327684 | tf_op jit(solution)/shard_map/dot_general | solution.py:37
  136.3 0.6 multiply_reduce_fusion.1
  137.6 5.4 %while.21 = (s32[]{:T(128)}, f32[128,128]{1,0:T(8,128)S(1)}, s32[]{:T(128)}) while((s32[]{:T(128)}, f32[128,128]{1,0:T(8,128)S(1)}, s32[]{:T(128)}) %tuple.50), condition=%wide.region_4.5_spmd, body=%wide.region_3.4_spmd.sunk | while | flops 50380800 | bytes 458797 | solution.py:50
  143.1 0.8 multiply_reduce_fusion
  144.8 9.0 %while.22 = (s32[]{:T(128)}, f32[256,128]{0,1:T(8,128)S(1)}, s32[]{:T(128)}) while((s32[]{:T(128)}, f32[256,128]{0,1:T(8,128)S(1)}, s32[]{:T(128)}) %tuple.53), condition=%wide.region_7.8_spmd.clone, body=%wide.region_6.7_spmd.clone.sunk | while | flops 75563008 | bytes 786477 | solution.py:60
  146.4 0.3 convolution_bitcast_fusion.8
  147.0 0.3 convolution_bitcast_fusion.8
  148.3 0.3 convolution_bitcast_fusion.8
  149.0 0.3 convolution_bitcast_fusion.8
  150.3 0.3 convolution_bitcast_fusion.8
  150.9 0.3 convolution_bitcast_fusion.8
  152.2 0.3 convolution_bitcast_fusion.8
  152.8 0.3 convolution_bitcast_fusion.8
  154.1 0.4 fusion.204
  154.5 1.5 fusion.12
  156.0 1.6 %convolution_subtract_fusion.2 = f32[256,512]{1,0:T(8,128)S(1)} fusion(f32[256,128]{1,0:T(8,128)S(1)} %fusion.204, f32[128,512]{1,0:T(8,128)S(1)} %fusion.12, f32[32,8,4,128]{3,2,1,0:T(4,128)S(1)} %all_to_all.25, f32[256,4,128]{2,1,0:T(4,128)} %param.12), kind=kOutput, calls=%fused_computation.11 | convolution fusion | flops 201719808 | bytes 1966080 | tf_op jit(solution)/shard_map/dot_general | solution.py:37
  157.7 1.0 reshape.93
  (109 shorter events, 12.6 us)
Async XLA Ops:
  0.6 20.2 %copy-start = (f32[8,4,128,128]{3,2,1,0:T(8,128)S(1)}, f32[8,4,128,128]{3,2,1,0:T(8,128)}, u32[]{:S(2)}) copy-start(f32[8,4,128,128]{3,2,1,0:T(8,128)} %param.14) | copy-start | bytes 6291460
  0.6 11.5 %copy-start.3 = (f32[8,4,4096]{2,1,0:T(4,128)S(1)}, f32[8,4,4096]{2,1,0:T(4,128)}, u32[]{:S(2)}) copy-start(f32[8,4,4096]{2,1,0:T(4,128)} %param.11) | copy-start | bytes 1572868
  3.0 14.9 %copy-start.6 = (s32[8,4]{0,1:T(4,128)S(1)}, s32[8,4]{0,1:T(4,128)}, u32[]{:S(2)}) copy-start(s32[8,4]{0,1:T(4,128)} %param.15) | copy-start | bytes 388
  3.0 38.4 %all-to-all-start = ((f32[8,8,2,4,4,128]{5,3,4,1,2,0:T(4,128)}), f32[8,8,2,4,4,128]{5,3,4,1,2,0:T(4,128)}, u32[]{:S(2)}, u32[]{:S(2)}) async-start(f32[8,8,2,4,4,128]{5,3,4,1,2,0:T(4,128)} %broadcast_in_dim.8), calls=%async_computation | async-start | bytes 2097152 | tf_op jit(solution)/shard_map/all_to_all | solution.py:140
  12.1 7.7 %copy-start.7 = (s32[8,4]{0,1:T(4,128)S(1)}, s32[8,4]{0,1:T(4,128)}, u32[]{:S(2)}) copy-start(s32[8,4]{0,1:T(4,128)} %param.16) | copy-start | bytes 388
  13.2 51.3 %collective-permute-start = (f32[32,8,1,128]{3,0,2,1:T(8,128)}, f32[32,8,1,128]{3,0,2,1:T(8,128)S(1)}, u32[]{:S(2)}, u32[]{:S(2)}) collective-permute-start(f32[32,8,1,128]{3,0,2,1:T(8,128)} %get-tuple-element.61), channel_id=1, source_target_pairs={{0,32},{32,64},{64,96},{96,128},{128,160},{160,192},{192,224},{1,3... | collective-permute-start | bytes 393224 | tf_op jit(solution)/shard_map/ppermute | solution.py:28
  16.5 47.9 %collective-permute-start.1 = (f32[32,8,1,128]{3,0,2,1:T(8,128)}, f32[32,8,1,128]{3,0,2,1:T(8,128)}, u32[]{:S(2)}, u32[]{:S(2)}) collective-permute-start(f32[32,8,1,128]{3,0,2,1:T(8,128)} %get-tuple-element.62), channel_id=1, source_target_pairs={{32,0},{64,32},{96,64},{128,96},{160,128},{192,160},{224,192},{33,... | collective-permute-start | bytes 393224 | tf_op jit(solution)/shard_map/ppermute | solution.py:31
  41.4 23.1 %all-to-all-start.1 = ((f32[32,8,4,128]{3,2,1,0:T(4,128)}), f32[32,8,4,128]{3,2,1,0:T(4,128)S(1)}, u32[]{:S(2)}, u32[]{:S(2)}) async-start(f32[32,8,4,128]{3,2,1,0:T(4,128)} %bitcast.38), calls=%async_computation.1 | async-start | bytes 1048576 | tf_op jit(solution)/shard_map/all_to_all | solution.py:217
  67.5 20.8 %copy-start.5 = (bf16[4,128,128]{2,1,0:T(8,128)(2,1)S(1)}, bf16[4,128,128]{2,1,0:T(8,128)(2,1)}, u32[]{:S(2)}) copy-start(bf16[4,128,128]{2,1,0:T(8,128)(2,1)} %param.13) | copy-start | bytes 393220
  89.9 20.4 %copy-start.2 = (f32[8,4,32,128]{3,2,1,0:T(8,128)S(1)}, f32[8,4,32,128]{3,2,1,0:T(8,128)}, u32[]{:S(2)}) copy-start(f32[8,4,32,128]{3,2,1,0:T(8,128)} %get-tuple-element.58) | copy-start | bytes 1572868
  105.9 14.1 %all-to-all-start.4 = ((f32[32,8,384]{2,1,0:T(8,128)}), f32[32,8,384]{2,1,0:T(8,128)S(1)}, u32[]{:S(2)}, u32[]{:S(2)}) async-start(f32[32,8,384]{2,1,0:T(8,128)} %broadcast_in_dim.10), calls=%async_computation.4 | async-start | bytes 786432 | tf_op jit(solution)/shard_map/all_to_all | solution.py:134
  132.5 12.1 %copy-start.4 = (f32[128,128]{1,0:T(8,128)S(1)}, f32[128,128]{1,0:T(8,128)}, u32[]{:S(2)}) copy-start(f32[128,128]{1,0:T(8,128)} %fusion.47) | copy-start | bytes 196612
  144.8 9.3 %copy-start.1 = (f32[128,256]{1,0:T(8,128)S(1)}, f32[128,256]{1,0:T(8,128)}, u32[]{:S(2)}) copy-start(f32[128,256]{1,0:T(8,128)} %shard_map.86) | copy-start | bytes 393220

commit v5 on v4

--- a/solution.py
+++ b/solution.py
@@ -44,8 +44,11 @@
     shifted = gram_mat - thresh_sq * identity
     signum = shifted / jnp.sqrt(jnp.sum(shifted * shifted))
 
+    def iter_mm(first_mat, second_mat):
+        return jnp.dot(first_mat, second_mat, precision=lax.Precision.HIGH)
+
     def sign_step(turn_no, current):
-        return 1.5 * current - 0.5 * matmul_hi(matmul_hi(current, current), current)
+        return 1.5 * current - 0.5 * iter_mm(iter_mm(current, current), current)
 
     signum = lax.fori_loop(0, SIGN_ITERS, sign_step, signum)
     keeper = 0.5 * (identity + signum)
@@ -54,8 +57,8 @@
 
     def root_step(turn_no, stacked):
         root_iter, inv_iter = stacked[:order_n], stacked[order_n:]
-        step_mat = 0.5 * (3.0 * identity - matmul_hi(inv_iter, root_iter))
-        return matmul_hi(stacked, step_mat)
+        step_mat = 0.5 * (3.0 * identity - iter_mm(inv_iter, root_iter))
+        return iter_mm(stacked, step_mat)
 
     stacked = lax.fori_loop(
         0, ROOT_ITERS, root_step, jnp.concatenate([floored / scale_c, identity], axis=0)
@@ -132,12 +135,6 @@
     mine = jnp.sum(lax.all_to_all(pieces, axis, 0, 0, tiled=True), axis=0)
     spread = jnp.broadcast_to(mine[None], pieces.shape)
     return lax.all_to_all(spread, axis, 0, 0, tiled=True).reshape(value.shape)
-
-
-def exchange_gather(value, axis):
-    count = lax.axis_size(axis)
-    spread = jnp.broadcast_to(value[None], (count,) + value.shape)
-    return lax.all_to_all(spread, axis, 0, 0, tiled=True)
 
 
 def data_gradient(sky_b, grid_tiles, freq_block, vis_block, vis_all):
@@ -217,7 +214,7 @@
     dual_b = lax.all_to_all(
         dual_field.reshape(blocks_n, chan_count, row_count, block), "chan", 0, 0, tiled=True
     )
-    vis_all = exchange_gather(vis_data, "facet")
+    vis_all = lax.all_gather(vis_data, "facet", axis=0)
     sky_b = jnp.transpose(sky_image.reshape(chan_count, row_count, blocks_n, block), (2, 0, 1, 3))
     padded = padded_2(sky_b, (("facet", 2),), 1)
     grad_b = data_gradient(sky_b, grid_tiles, freq_block, vis_block, vis_all)

time: 159 us -> 169 us (1.063)
  between operations: 3.21 us -> 16.3 us
  starting transfers between devices: 25.3 us -> 17.4 us
  matrix products: 49.5 us -> 44.7 us
  blocking collectives: 32.8 us -> 36.5 us
  local copies, waits for them, and re-layouts: 10 us -> 13.7 us
    all_gather x0 -> x1, waiting for transfers between devices: none -> 17.5 us  [_on_device(): vis_all = lax.all_gather(vis_data, 'facet', axis=0)]
    all_to_all x1 -> x0, waiting for transfers between devices: 15.7 us -> none  [exchange_gather(): return lax.all_to_all(spread, axis, 0, 0, tiled=True)]
    dot_general x69 -> x17, matrix products: 27.1 us -> 12.4 us  [matmul_hi(): return jnp.dot(first_mat, second_mat, precision=HI)]
    dot_general x0 -> x52, matrix products: none -> 11.4 us  [iter_mm(): return jnp.dot(first_mat, second_mat, precision=lax.Precision.HIGH)]
    all_to_all x1 -> x0, starting transfers between devices: 9.13 us -> none  [exchange_gather(): return lax.all_to_all(spread, axis, 0, 0, tiled=True)]
    all_to_all x1, blocking collectives: 18.6 us -> 22.3 us  [_on_device(): lax.all_to_all(rest, 'chan', 0, 0, tiled=True).reshape(dual_field.shape)]
    all_gather x0 -> x1, local copies, waits for them, and re-layouts: none -> 1.84 us  [_on_device(): vis_all = lax.all_gather(vis_data, 'facet', axis=0)]
  transfers between devices with their start and end apart: 5 -> 5, of which waited for: 2 -> 2; matrix products, arithmetic and copies ran while one was open for 16% -> 17% of each run, Pallas kernels for 0% -> 0%
where the time goes in v5:
time: 169 us; the launch traced here: 168 us
  matrix products  44.7 us (26%)
  blocking collectives  36.5 us (22%)
  waiting for transfers between devices  25.7 us (15%)
  starting transfers between devices  17.4 us (10%)
  between operations  16.3 us (10%)
  local copies, waits for them, and re-layouts  13.7 us (8%)
  Pallas kernels  10.8 us (6%)
  other arithmetic  1.72 us (1%)
    all_to_all x1, blocking collectives, _on_device(): lax.all_to_all(rest, 'chan', 0, 0, tiled=True).reshape(dual_field.shape)  22.3 us
    all_gather x1, waiting for transfers between devices, _on_device(): vis_all = lax.all_gather(vis_data, 'facet', axis=0)  17.5 us
    all_to_all x1, blocking collectives, exchange_sum(): mine = jnp.sum(lax.all_to_all(pieces, axis, 0, 0, tiled=True), axis=0)  14.2 us
    dot_general x17, matrix products, matmul_hi(): return jnp.dot(first_mat, second_mat, precision=HI)  12.4 us
    dot_general x52, matrix products, iter_mm(): return jnp.dot(first_mat, second_mat, precision=lax.Precision.HIGH)  11.4 us
    pallas_call x1, Pallas kernels, basis_transposed(): pl.pallas_call(_basis_kernel, out_shape=jax.ShapeDtypeStruct(side.shape,...  10.8 us
    all_to_all x1, starting transfers between devices, _on_device(): lax.all_to_all(dual_field.reshape(blocks_n, chan_count, row_count, block)...  8.65 us
    all_to_all x1, waiting for transfers between devices, exchange_sum(): return lax.all_to_all(spread, axis, 0, 0, tiled=True).reshape(value.shape)  7.55 us
  transfers between devices with their start and end apart: 5, of which 2 were waited for; matrix products, arithmetic and copies ran while one was open for 17% of the time, Pallas kernels for 0%

profile of v5, /device:TPU:1, one launch (start us, length us, event | category | flops | bytes accessed | tf_op | source)
XLA Modules:
  0.0 167.8 jit_solution(8199646125855811841)
XLA Ops:
  7.2 0.7 all-gather.3.cloned.1.call-update
  7.9 8.6 %all-to-all-start = ((f32[32,8,4,128]{3,2,1,0:T(4,128)}), f32[32,8,4,128]{3,2,1,0:T(4,128)}, u32[]{:S(2)}, u32[]{:S(2)}) async-start(f32[32,8,4,128]{3,2,1,0:T(4,128)} %bitcast.166), calls=%async_computation | async-start | bytes 1048576 | tf_op jit(solution)/shard_map/all_to_all | solution.py:214
  16.6 1.4 reshape.77
  18.0 0.7 fusion.196
  18.7 3.5 %collective-permute-start = (f32[32,8,1,128]{3,0,2,1:T(8,128)}, f32[32,8,1,128]{3,0,2,1:T(8,128)S(1)}, u32[]{:S(2)}, u32[]{:S(2)}) collective-permute-start(f32[32,8,1,128]{3,0,2,1:T(8,128)} %get-tuple-element.61), channel_id=1, source_target_pairs={{0,32},{32,64},{64,96},{96,128},{128,160},{160,192},{192,224},{1,3... | collective-permute-start | bytes 393224 | tf_op jit(solution)/shard_map/ppermute | solution.py:28
  22.3 1.3 collective-permute-start.1
  23.9 0.6 convolution_negate_fusion
  24.4 0.6 multiply_subtract_fusion.1
  25.0 0.5 fusion.71
  25.6 0.5 fusion.75
  26.1 0.5 fusion.11
  26.6 1.9 %fusion.202 = f32[8,4,4,128]{3,2,1,0:T(4,128)S(1)} fusion(f32[8,4,4,128]{3,2,1,0:T(4,128)S(1)} %bitcast.183, f32[8,4,128,128]{3,2,1,0:T(8,128)S(1)} %copy-done), kind=kOutput, calls=%fused_computation.233 | convolution fusion | flops 25165824 | bytes 2228224 | tf_op jit(solution)/shard_map/ctrj,ctjm->ctrm/dot_general | solution.py:188
  28.4 0.3 fusion.43
  28.8 0.5 fusion.10
  29.2 1.9 %fusion.203 = f32[8,4,4,128]{3,2,1,0:T(4,128)S(1)} fusion(f32[8,4,4,128]{3,2,1,0:T(4,128)S(1)} %bitcast.184, f32[8,4,128,128]{3,2,1,0:T(8,128)S(1)} %copy-done), kind=kOutput, calls=%fused_computation.234 | convolution fusion | flops 25165824 | bytes 2228224 | tf_op jit(solution)/shard_map/ctrj,ctjm->ctrm/dot_general | solution.py:189
  31.1 0.3 fusion.36
  31.4 17.5 %all-gather.3.cloned.1.call-done = f32[64,2,4,4,128]{4,3,2,1,0:T(4,128)} async-done(((f32[8,2,4,4,128]{4,3,2,1,0:T(4,128)}), f32[64,2,4,4,128]{4,3,2,1,0:T(4,128)}) %all-gather.3.cloned.1.call-update) | async-done | bytes 1048592 | tf_op jit(solution)/shard_map/all_gather | solution.py:217
  48.9 1.8 %copy.244 = f32[64,2,4,4,128]{4,0,3,2,1:T(8,128)S(1)} copy(f32[64,2,4,4,128]{4,3,2,1,0:T(4,128)} %all-gather.3.cloned.1.call-done) | data formatting | bytes 2097152 | tf_op jit(solution)/shard_map/all_gather | solution.py:217
  50.8 0.7 convolution_bitcast_fusion.4
  51.5 0.7 convolution_bitcast_fusion.6
  52.1 0.7 convolution_bitcast_fusion.3
  52.8 0.7 convolution_bitcast_fusion.5
  53.8 3.5 %fusion.38 = f32[8,4,4,128]{3,2,1,0:T(4,128)S(1)} fusion(f32[8,4,128,128]{3,2,1,0:T(8,128)S(1)} %copy-done, f32[8,4,4,128]{3,1,2,0:T(4,128)S(1)} %fusion.40), kind=kOutput, calls=%fused_computation.74 | convolution fusion | flops 25165824 | bytes 2228224 | tf_op jit(solution)/shard_map/ctrm,ctjm->ctrj/dot_general | solution.py:195
  57.6 3.4 %fusion.31 = f32[8,4,4,128]{3,2,1,0:T(4,128)S(1)} fusion(f32[8,4,128,128]{3,2,1,0:T(8,128)S(1)} %copy-done, f32[8,4,4,128]{3,1,2,0:T(4,128)S(1)} %fusion.33), kind=kOutput, calls=%fused_computation.66 | convolution fusion | flops 25165824 | bytes 2228224 | tf_op jit(solution)/shard_map/ctrm,ctjm->ctrj/dot_general | solution.py:196
  61.0 0.5 fusion.73
  61.5 0.5 fusion.9
  61.9 0.5 fusion.77
  62.4 0.5 fusion.8
  62.9 1.6 fusion.52
  64.5 3.3 %multiply_subtract_fusion = (f32[32,8,4,128]{3,0,2,1:T(8,128)S(1)}, f32[8,4,32,128]{3,2,1,0:T(8,128)}) fusion(f32[32,8,4,128]{3,0,2,1:T(8,128)S(1)} %bitcast.168, f32[32,8,1,128]{3,0,2,1:T(8,128)} %collective-permute-done.1, f32[32,8,1,128]{3,0,2,1:T(8,128)S(1)} %collective-permute-done, f32[32,8,4,128]{3,2,1,0:T(4,128)} %all-to-all-done, ...), kind=kOutput, calls=%fused_computation.46 | convolution fusion | flops 8189952 | bytes 3047552 | tf_op jit(solution)/shard_map/ctn,ctrm->ncrm/dot_general | solution.py:205
  67.7 0.3 copy.132
  68.1 22.3 %all_to_all.20 = f32[32,8,4,128]{3,2,1,0:T(4,128)S(1)} all-to-all(f32[32,8,4,128]{3,2,1,0:T(4,128)S(1)} %copy.132), channel_id=1, replica_groups=mesh['facet'=8,'chan'=32] {'chan'}, dimensions={0} | all-to-all | bytes 1048576 | tf_op jit(solution)/shard_map/all_to_all | solution.py:227
  90.4 0.7 convolution_bitcast_fusion.1
  91.0 0.5 convolution_bitcast_fusion.2
  91.6 0.9 copy.136
  92.5 14.2 %all_to_all.21 = f32[32,8,384]{2,1,0:T(8,128)S(1)} all-to-all(f32[32,8,384]{2,1,0:T(8,128)} %bitcast.173), channel_id=1, replica_groups=mesh['facet'=8,'chan'=32] {'chan'}, dimensions={0} | all-to-all | bytes 786432 | tf_op jit(solution)/shard_map/all_to_all | solution.py:135
  106.7 0.8 broadcast_in_dim.7
  107.5 3.9 %all-to-all-start.3 = ((f32[32,8,384]{2,1,0:T(8,128)}), f32[32,8,384]{2,1,0:T(8,128)S(1)}, u32[]{:S(2)}, u32[]{:S(2)}) async-start(f32[32,8,384]{2,1,0:T(8,128)} %broadcast_in_dim.7), calls=%async_computation.3 | async-start | bytes 786432 | tf_op jit(solution)/shard_map/all_to_all | solution.py:137
  111.4 0.6 fusion.47
  112.0 2.0 %reshape.87 = f32[8,4,4096]{2,1,0:T(4,128)} reshape(f32[8,4,32,128]{3,2,1,0:T(8,128)} %get-tuple-element.58) | data formatting | bytes 1048576 | tf_op jit(solution)/shard_map/reshape | solution.py:223
  114.0 7.5 %all-to-all-done.3 = f32[32,8,384]{2,1,0:T(8,128)S(1)} async-done(((f32[32,8,384]{2,1,0:T(8,128)}), f32[32,8,384]{2,1,0:T(8,128)S(1)}, u32[]{:S(2)}, u32[]{:S(2)}) %all-to-all-start.3) | async-done | bytes 393248 | tf_op jit(solution)/shard_map/all_to_all | solution.py:137
  121.5 1.0 fusion.188.gram_ref
  122.6 0.7 slice.50
  123.2 1.7 copy.159
  124.9 10.8 %shard_map.86 = f32[128,256]{1,0:T(8,128)} custom-call(f32[128,128]{1,0:T(8,128)} %fusion.188.gram_ref, f32[128,256]{1,0:T(8,128)} %bitcast.174), custom_call_target="tpu_custom_call" | custom-call | flops 25165824 | bytes 327680 | tf_op jit(solution)/shard_map/pallas_call | solution.py:109
  135.7 1.3 fusion.22
  137.0 1.8 %select_reduce_fusion = (f32[]{:T(128)}, f32[128,128]{1,0:T(8,128)S(1)}) fusion(f32[128,256]{1,0:T(8,128)} %shard_map.86, f32[256,128]{1,0:T(8,128)S(1)} %fusion.22), kind=kOutput, calls=%fused_computation.86 | convolution fusion | flops 50380800 | bytes 327684 | tf_op jit(solution)/shard_map/dot_general | solution.py:37
  139.4 0.6 multiply_reduce_fusion.1
  140.6 4.8 %while.21 = (s32[]{:T(128)}, f32[128,128]{1,0:T(8,128)S(1)}, s32[]{:T(128)}) while((s32[]{:T(128)}, f32[128,128]{1,0:T(8,128)S(1)}, s32[]{:T(128)}) %tuple.50), condition=%wide.region_4.5_spmd, body=%wide.region_3.4_spmd.sunk | while | flops 25214976 | bytes 458797 | solution.py:53
  145.4 0.8 multiply_reduce_fusion
  147.0 7.8 %while.22 = (s32[]{:T(128)}, f32[256,128]{0,1:T(8,128)S(1)}, s32[]{:T(128)}) while((s32[]{:T(128)}, f32[256,128]{0,1:T(8,128)S(1)}, s32[]{:T(128)}) %tuple.53), condition=%wide.region_7.8_spmd.clone, body=%wide.region_6.7_spmd.clone.sunk | while | flops 37814272 | bytes 786477 | solution.py:63
  147.3 0.3 convolution_bitcast_fusion.8
  147.9 0.3 convolution_bitcast_fusion.8
  148.4 0.3 convolution_bitcast_fusion.8
  149.0 0.3 convolution_bitcast_fusion.8
  149.6 0.3 convolution_bitcast_fusion.8
  152.3 0.3 convolution_bitcast_fusion.8
  154.6 0.3 convolution_bitcast_fusion.8
  154.9 0.8 copy.139
  155.6 1.1 fusion.29
  156.7 0.4 fusion.204
  157.1 0.5 fusion.12
  157.6 1.4 convolution_subtract_fusion.2
  159.0 2.0 %reshape.92 = f32[256,4,128]{2,1,0:T(4,128)} reshape(f32[256,512]{1,0:T(8,128)} %convolution_subtract_fusion.2) | data formatting | bytes 1048576 | tf_op jit(solution)/shard_map/reshape | solution.py:244
  (107 shorter events, 11.2 us)
Async XLA Ops:
  7.2 19.4 %copy-start = (f32[8,4,128,128]{3,2,1,0:T(8,128)S(1)}, f32[8,4,128,128]{3,2,1,0:T(8,128)}, u32[]{:S(2)}) copy-start(f32[8,4,128,128]{3,2,1,0:T(8,128)} %param.14) | copy-start | bytes 6291460
  7.2 16.4 %copy-start.5 = (s32[8,4]{0,1:T(4,128)S(1)}, s32[8,4]{0,1:T(4,128)}, u32[]{:S(2)}) copy-start(s32[8,4]{0,1:T(4,128)} %param.15) | copy-start | bytes 388
  7.2 41.7 %all-gather.3.cloned.1.call-start = ((), (), s32[]{:S(2)}) async-start(), calls=%async_computation.4 | async-start | bytes 1179648 | tf_op jit(solution)/shard_map/all_gather | solution.py:217
  7.9 17.6 %copy-start.6 = (s32[8,4]{0,1:T(4,128)S(1)}, s32[8,4]{0,1:T(4,128)}, u32[]{:S(2)}) copy-start(s32[8,4]{0,1:T(4,128)} %param.16) | copy-start | bytes 388
  7.9 56.5 %all-to-all-start = ((f32[32,8,4,128]{3,2,1,0:T(4,128)}), f32[32,8,4,128]{3,2,1,0:T(4,128)}, u32[]{:S(2)}, u32[]{:S(2)}) async-start(f32[32,8,4,128]{3,2,1,0:T(4,128)} %bitcast.166), calls=%async_computation | async-start | bytes 1048576 | tf_op jit(solution)/shard_map/all_to_all | solution.py:214
  18.7 45.7 %collective-permute-start = (f32[32,8,1,128]{3,0,2,1:T(8,128)}, f32[32,8,1,128]{3,0,2,1:T(8,128)S(1)}, u32[]{:S(2)}, u32[]{:S(2)}) collective-permute-start(f32[32,8,1,128]{3,0,2,1:T(8,128)} %get-tuple-element.61), channel_id=1, source_target_pairs={{0,32},{32,64},{64,96},{96,128},{128,160},{160,192},{192,224},{1,3... | collective-permute-start | bytes 393224 | tf_op jit(solution)/shard_map/ppermute | solution.py:28
  22.3 42.2 %collective-permute-start.1 = (f32[32,8,1,128]{3,0,2,1:T(8,128)}, f32[32,8,1,128]{3,0,2,1:T(8,128)}, u32[]{:S(2)}, u32[]{:S(2)}) collective-permute-start(f32[32,8,1,128]{3,0,2,1:T(8,128)} %get-tuple-element.62), channel_id=1, source_target_pairs={{32,0},{64,32},{96,64},{128,96},{160,128},{192,160},{224,192},{33,... | collective-permute-start | bytes 393224 | tf_op jit(solution)/shard_map/ppermute | solution.py:31
  64.4 25.9 %copy-start.1 = (f32[256,4,128]{2,1,0:T(4,128)S(1)}, f32[256,4,128]{2,1,0:T(4,128)}, u32[]{:S(2)}) copy-start(f32[256,4,128]{2,1,0:T(4,128)} %param.12) | copy-start | bytes 1572868
  67.7 23.3 %copy-start.4 = (bf16[4,128,128]{2,1,0:T(8,128)(2,1)S(1)}, bf16[4,128,128]{2,1,0:T(8,128)(2,1)}, u32[]{:S(2)}) copy-start(bf16[4,128,128]{2,1,0:T(8,128)(2,1)} %param.13) | copy-start | bytes 393220
  107.5 14.1 %all-to-all-start.3 = ((f32[32,8,384]{2,1,0:T(8,128)}), f32[32,8,384]{2,1,0:T(8,128)S(1)}, u32[]{:S(2)}, u32[]{:S(2)}) async-start(f32[32,8,384]{2,1,0:T(8,128)} %broadcast_in_dim.7), calls=%async_computation.3 | async-start | bytes 786432 | tf_op jit(solution)/shard_map/all_to_all | solution.py:137
  136.9 10.0 %copy-start.3 = (f32[128,128]{1,0:T(8,128)S(1)}, f32[128,128]{1,0:T(8,128)}, u32[]{:S(2)}) copy-start(f32[128,128]{1,0:T(8,128)} %fusion.47) | copy-start | bytes 196612
  147.0 9.6 %copy-start.2 = (f32[128,256]{1,0:T(8,128)S(1)}, f32[128,256]{1,0:T(8,128)}, u32[]{:S(2)}) copy-start(f32[128,256]{1,0:T(8,128)} %shard_map.86) | copy-start | bytes 393220
Sparse Core Ops, SparseCore 0:
  9.8 39.0 all-gather.2

commit v6 on v5

--- a/solution.py
+++ b/solution.py
@@ -50,7 +50,7 @@
     def sign_step(turn_no, current):
         return 1.5 * current - 0.5 * iter_mm(iter_mm(current, current), current)
 
-    signum = lax.fori_loop(0, SIGN_ITERS, sign_step, signum)
+    signum = lax.fori_loop(0, SIGN_ITERS, sign_step, signum, unroll=True)
     keeper = 0.5 * (identity + signum)
     floored = 0.5 * (gram_mat + thresh_sq * identity + matmul_hi(shifted, signum))
     scale_c = jnp.sqrt(jnp.sum(floored * floored))
@@ -61,7 +61,7 @@
         return iter_mm(stacked, step_mat)
 
     stacked = lax.fori_loop(
-        0, ROOT_ITERS, root_step, jnp.concatenate([floored / scale_c, identity], axis=0)
+        0, ROOT_ITERS, root_step, jnp.concatenate([floored / scale_c, identity], axis=0), unroll=True
     )
     inv_iter = stacked[order_n:]
     inv_root = inv_iter / jnp.sqrt(scale_c)
@@ -135,6 +135,12 @@
     mine = jnp.sum(lax.all_to_all(pieces, axis, 0, 0, tiled=True), axis=0)
     spread = jnp.broadcast_to(mine[None], pieces.shape)
     return lax.all_to_all(spread, axis, 0, 0, tiled=True).reshape(value.shape)
+
+
+def exchange_gather(value, axis):
+    count = lax.axis_size(axis)
+    spread = jnp.broadcast_to(value[None], (count,) + value.shape)
+    return lax.all_to_all(spread, axis, 0, 0, tiled=True)
 
 
 def data_gradient(sky_b, grid_tiles, freq_block, vis_block, vis_all):
@@ -214,7 +220,7 @@
     dual_b = lax.all_to_all(
         dual_field.reshape(blocks_n, chan_count, row_count, block), "chan", 0, 0, tiled=True
     )
-    vis_all = lax.all_gather(vis_data, "facet", axis=0)
+    vis_all = exchange_gather(vis_data, "facet")
     sky_b = jnp.transpose(sky_image.reshape(chan_count, row_count, blocks_n, block), (2, 0, 1, 3))
     padded = padded_2(sky_b, (("facet", 2),), 1)
     grad_b = data_gradient(sky_b, grid_tiles, freq_block, vis_block, vis_all)

time: 169 us -> 155 us (0.917)
  between operations: 16.3 us -> 3.57 us
  starting transfers between devices: 17.4 us -> 25.3 us
  local copies, waits for them, and re-layouts: 13.7 us -> 9.64 us
  blocking collectives: 36.5 us -> 32.8 us
    all_gather x1 -> x0, waiting for transfers between devices: 17.5 us -> none  [_on_device(): vis_all = lax.all_gather(vis_data, 'facet', axis=0)]
    all_to_all x0 -> x1, waiting for transfers between devices: none -> 15.7 us  [exchange_gather(): return lax.all_to_all(spread, axis, 0, 0, tiled=True)]
    all_to_all x0 -> x1, starting transfers between devices: none -> 9.13 us  [exchange_gather(): return lax.all_to_all(spread, axis, 0, 0, tiled=True)]
    all_to_all x1, blocking collectives: 22.3 us -> 18.6 us  [_on_device(): lax.all_to_all(rest, 'chan', 0, 0, tiled=True).reshape(dual_field.shape)]
    all_gather x1 -> x0, local copies, waits for them, and re-layouts: 1.84 us -> none  [_on_device(): vis_all = lax.all_gather(vis_data, 'facet', axis=0)]
    dot_general x52, matrix products: 11.4 us -> 9.53 us  [iter_mm(): return jnp.dot(first_mat, second_mat, precision=lax.Precision.HIGH)]
where the time goes in v6:
time: 155 us; the launch traced here: 154 us
  matrix products  45.8 us (30%)
  blocking collectives  32.8 us (21%)
  starting transfers between devices  25.3 us (16%)
  waiting for transfers between devices  24.4 us (16%)
  Pallas kernels  10.8 us (7%)
  local copies, waits for them, and re-layouts  9.64 us (6%)
  between operations  3.57 us (2%)
  other arithmetic  1.69 us (1%)
    all_to_all x1, blocking collectives, _on_device(): lax.all_to_all(rest, 'chan', 0, 0, tiled=True).reshape(dual_field.shape)  18.6 us
    all_to_all x1, waiting for transfers between devices, exchange_gather(): return lax.all_to_all(spread, axis, 0, 0, tiled=True)  15.7 us
    all_to_all x1, blocking collectives, exchange_sum(): mine = jnp.sum(lax.all_to_all(pieces, axis, 0, 0, tiled=True), axis=0)  14.2 us
    dot_general x17, matrix products, matmul_hi(): return jnp.dot(first_mat, second_mat, precision=HI)  13.8 us
    pallas_call x1, Pallas kernels, basis_transposed(): pl.pallas_call(_basis_kernel, out_shape=jax.ShapeDtypeStruct(side.shape,...  10.8 us
    dot_general x52, matrix products, iter_mm(): return jnp.dot(first_mat, second_mat, precision=lax.Precision.HIGH)  9.53 us
    all_to_all x1, starting transfers between devices, exchange_gather(): return lax.all_to_all(spread, axis, 0, 0, tiled=True)  9.13 us
    all_to_all x1, waiting for transfers between devices, exchange_sum(): return lax.all_to_all(spread, axis, 0, 0, tiled=True).reshape(value.shape)  8.66 us
  transfers between devices with their start and end apart: 5, of which 2 were waited for; matrix products, arithmetic and copies ran while one was open for 17% of the time, Pallas kernels for 0%

profile of v6, /device:TPU:1, one launch (start us, length us, event | category | flops | bytes accessed | tf_op | source)
XLA Modules:
  0.0 153.9 jit_solution(2638132925498633039)
XLA Ops:
  0.7 1.1 copy.102
  1.8 1.2 broadcast_in_dim.8
  3.0 9.1 %all-to-all-start = ((f32[8,8,2,4,4,128]{5,3,4,1,2,0:T(4,128)}), f32[8,8,2,4,4,128]{5,3,4,1,2,0:T(4,128)}, u32[]{:S(2)}, u32[]{:S(2)}) async-start(f32[8,8,2,4,4,128]{5,3,4,1,2,0:T(4,128)} %broadcast_in_dim.8), calls=%async_computation | async-start | bytes 2097152 | tf_op jit(solution)/shard_map/all_to_all | solution.py:143
  12.1 0.4 reshape.78
  12.5 0.7 fusion.250
  13.2 3.3 %collective-permute-start = (f32[32,8,1,128]{3,0,2,1:T(8,128)}, f32[32,8,1,128]{3,0,2,1:T(8,128)S(1)}, u32[]{:S(2)}, u32[]{:S(2)}) collective-permute-start(f32[32,8,1,128]{3,0,2,1:T(8,128)} %get-tuple-element.6), channel_id=1, source_target_pairs={{0,32},{32,64},{64,96},{96,128},{128,160},{160,192},{192,224},{1,3... | collective-permute-start | bytes 393224 | tf_op jit(solution)/shard_map/ppermute | solution.py:28
  16.5 1.3 collective-permute-start.1
  17.9 0.2 fusion.158
  18.2 0.6 convolution_negate_fusion
  18.7 0.6 multiply_subtract_fusion.1
  19.3 0.5 fusion.120
  19.9 0.5 fusion.124
  20.4 0.5 fusion.32
  20.8 1.9 %fusion.256 = f32[8,4,4,128]{3,2,1,0:T(4,128)S(1)} fusion(f32[8,4,4,128]{3,2,1,0:T(4,128)S(1)} %bitcast.229, f32[8,4,128,128]{3,2,1,0:T(8,128)S(1)} %copy-done), kind=kOutput, calls=%fused_computation.307 | convolution fusion | flops 25165824 | bytes 2228224 | tf_op jit(solution)/shard_map/ctrj,ctjm->ctrm/dot_general | solution.py:195
  22.7 0.3 fusion.83
  23.0 0.5 fusion.33
  23.5 1.9 %fusion.255 = f32[8,4,4,128]{3,2,1,0:T(4,128)S(1)} fusion(f32[8,4,4,128]{3,2,1,0:T(4,128)S(1)} %bitcast.230, f32[8,4,128,128]{3,2,1,0:T(8,128)S(1)} %copy-done), kind=kOutput, calls=%fused_computation.306 | convolution fusion | flops 25165824 | bytes 2228224 | tf_op jit(solution)/shard_map/ctrj,ctjm->ctrm/dot_general | solution.py:194
  25.4 0.3 fusion.90
  25.7 15.7 %all-to-all-done = f32[8,8,2,4,4,128]{5,3,4,1,2,0:T(4,128)} async-done(((f32[8,8,2,4,4,128]{5,3,4,1,2,0:T(4,128)}), f32[8,8,2,4,4,128]{5,3,4,1,2,0:T(4,128)}, u32[]{:S(2)}, u32[]{:S(2)}) %all-to-all-start) | async-done | bytes 1048608 | tf_op jit(solution)/shard_map/all_to_all | solution.py:143
  41.4 7.7 %all-to-all-start.1 = ((f32[32,8,4,128]{3,2,1,0:T(4,128)}), f32[32,8,4,128]{3,2,1,0:T(4,128)S(1)}, u32[]{:S(2)}, u32[]{:S(2)}) async-start(f32[32,8,4,128]{3,2,1,0:T(4,128)} %bitcast.38), calls=%async_computation.1 | async-start | bytes 1048576 | tf_op jit(solution)/shard_map/all_to_all | solution.py:220
  49.1 1.3 fusion.249
  50.4 0.8 convolution_bitcast_fusion.2
  51.2 0.8 convolution_bitcast_fusion.4
  52.0 0.8 convolution_bitcast_fusion.3
  52.8 0.8 convolution_bitcast_fusion.5
  53.7 0.3 fusion.80
  54.0 3.4 %fusion.78 = f32[8,4,4,128]{3,2,1,0:T(4,128)S(1)} fusion(f32[8,4,128,128]{3,2,1,0:T(8,128)S(1)} %copy-done, f32[8,4,4,128]{3,1,2,0:T(4,128)S(1)} %fusion.80), kind=kOutput, calls=%fused_computation.135 | convolution fusion | flops 25165824 | bytes 2228224 | tf_op jit(solution)/shard_map/ctrm,ctjm->ctrj/dot_general | solution.py:202
  57.4 0.3 fusion.87
  57.7 3.4 %fusion.85 = f32[8,4,4,128]{3,2,1,0:T(4,128)S(1)} fusion(f32[8,4,128,128]{3,2,1,0:T(8,128)S(1)} %copy-done, f32[8,4,4,128]{3,1,2,0:T(4,128)S(1)} %fusion.87), kind=kOutput, calls=%fused_computation.143 | convolution fusion | flops 25165824 | bytes 2228224 | tf_op jit(solution)/shard_map/ctrm,ctjm->ctrj/dot_general | solution.py:201
  61.0 0.5 fusion.122
  61.5 0.5 fusion.31
  62.0 0.5 fusion.126
  62.4 0.5 fusion.30
  62.9 1.6 %fusion.100 = f32[8,4,128,32]{2,3,1,0:T(8,128)} fusion(f32[8,4,4,128]{3,2,1,0:T(4,128)S(1)} %bitcast.223, f32[8,4,4,128]{3,2,1,0:T(4,128)S(1)} %bitcast.221, f32[8,4,128]{2,1,0:T(4,128)S(1)} %get-tuple-element.11, f32[8,4,128]{2,1,0:T(4,128)S(1)} %get-tuple-element.10, s32[8,4]{1,0:T(8,128)S(1)} %copy.96), kind=kOutput, calls=%fused_computation.163 | convolution fusion | flops 6354944 | bytes 688256 | tf_op jit(solution)/shard_map/ctn,ctrm->ncrm/dot_general | solution.py:211
  64.5 3.1 %multiply_subtract_fusion = (f32[32,8,4,128]{3,0,2,1:T(8,128)S(1)}, f32[8,4,32,128]{3,2,1,0:T(8,128)}) fusion(f32[32,8,4,128]{3,0,2,1:T(8,128)S(1)} %bitcast.215, f32[32,8,1,128]{3,0,2,1:T(8,128)} %collective-permute-done.1, f32[32,8,1,128]{3,0,2,1:T(8,128)S(1)} %collective-permute-done, f32[32,8,4,128]{3,2,1,0:T(4,128)S(1)} %all-to-all-done.1, ...), kind=kOutput, calls=%fused_computation.91 | convolution fusion | flops 8189952 | bytes 3047552 | tf_op jit(solution)/shard_map/ctn,ctrm->ncrm/dot_general | solution.py:211
  67.5 0.3 copy.125
  67.9 18.6 %all_to_all.25 = f32[32,8,4,128]{3,2,1,0:T(4,128)S(1)} all-to-all(f32[32,8,4,128]{3,2,1,0:T(4,128)S(1)} %copy.125), channel_id=1, replica_groups=mesh['facet'=8,'chan'=32] {'chan'}, dimensions={0} | all-to-all | bytes 1048576 | tf_op jit(solution)/shard_map/all_to_all | solution.py:233
  86.5 1.9 %convolution_bitcast_fusion = f32[256,256]{0,1:T(8,128)S(1)} fusion(f32[32,8,4,128]{3,2,1,0:T(4,128)S(1)} %all_to_all.25, f32[256,4,128]{2,1,0:T(4,128)} %param.8), kind=kOutput, calls=%fused_computation.3 | convolution fusion | flops 402915328 | bytes 1310720 | tf_op jit(solution)/shard_map/dot_general | solution.py:240
  88.4 1.5 convolution_bitcast_fusion.1
  90.0 0.9 copy.129
  90.9 14.2 %all_to_all.26 = f32[32,8,384]{2,1,0:T(8,128)S(1)} all-to-all(f32[32,8,384]{2,1,0:T(8,128)} %bitcast.219), channel_id=1, replica_groups=mesh['facet'=8,'chan'=32] {'chan'}, dimensions={0} | all-to-all | bytes 786432 | tf_op jit(solution)/shard_map/all_to_all | solution.py:135
  105.1 0.8 broadcast_in_dim.10
  105.9 3.8 %all-to-all-start.4 = ((f32[32,8,384]{2,1,0:T(8,128)}), f32[32,8,384]{2,1,0:T(8,128)S(1)}, u32[]{:S(2)}, u32[]{:S(2)}) async-start(f32[32,8,384]{2,1,0:T(8,128)} %broadcast_in_dim.10), calls=%async_computation.4 | async-start | bytes 786432 | tf_op jit(solution)/shard_map/all_to_all | solution.py:137
  109.7 0.6 fusion.95
  110.3 1.0 reshape.88
  111.3 8.7 %all-to-all-done.4 = f32[32,8,384]{2,1,0:T(8,128)S(1)} async-done(((f32[32,8,384]{2,1,0:T(8,128)}), f32[32,8,384]{2,1,0:T(8,128)S(1)}, u32[]{:S(2)}, u32[]{:S(2)}) %all-to-all-start.4) | async-done | bytes 393248 | tf_op jit(solution)/shard_map/all_to_all | solution.py:137
  120.0 1.0 fusion.242.gram_ref
  121.0 0.8 copy.150
  121.7 10.8 %shard_map.86 = f32[128,256]{1,0:T(8,128)} custom-call(f32[128,128]{1,0:T(8,128)} %fusion.242.gram_ref, f32[128,256]{1,0:T(8,128)} %bitcast.220), custom_call_target="tpu_custom_call" | custom-call | flops 25165824 | bytes 327680 | tf_op jit(solution)/shard_map/pallas_call | solution.py:109
  132.5 1.3 fusion.44
  133.8 1.8 %select_reduce_fusion = (f32[]{:T(128)}, f32[128,128]{1,0:T(8,128)S(1)}) fusion(f32[128,256]{1,0:T(8,128)} %shard_map.86, f32[256,128]{1,0:T(8,128)S(1)} %fusion.44), kind=kOutput, calls=%fused_computation.156 | convolution fusion | flops 50380800 | bytes 327684 | tf_op jit(solution)/shard_map/dot_general | solution.py:37
  136.3 0.6 multiply_reduce_fusion.1
  142.0 0.8 multiply_reduce_fusion
  143.8 0.2 fusion.46
  144.1 0.2 fusion.268
  144.5 0.2 fusion.269
  144.9 0.2 fusion.270
  145.3 0.2 fusion.271
  145.7 0.2 fusion.272
  149.1 0.2 fusion.92
  149.3 0.4 fusion.280
  149.7 1.5 fusion.34
  151.2 1.6 %convolution_subtract_fusion.1 = f32[256,512]{1,0:T(8,128)S(1)} fusion(f32[256,128]{1,0:T(8,128)S(1)} %fusion.280, f32[128,512]{1,0:T(8,128)S(1)} %fusion.34, f32[32,8,4,128]{3,2,1,0:T(4,128)S(1)} %all_to_all.25, f32[256,4,128]{2,1,0:T(4,128)} %param.8), kind=kOutput, calls=%fused_computation.2 | convolution fusion | flops 201719808 | bytes 1966080 | tf_op jit(solution)/shard_map/dot_general | solution.py:37
  152.9 1.0 reshape.93
  (77 shorter events, 8.8 us)
Async XLA Ops:
  0.6 20.2 %copy-start = (f32[8,4,128,128]{3,2,1,0:T(8,128)S(1)}, f32[8,4,128,128]{3,2,1,0:T(8,128)}, u32[]{:S(2)}) copy-start(f32[8,4,128,128]{3,2,1,0:T(8,128)} %param.10) | copy-start | bytes 6291460
  0.6 11.5 %copy-start.3 = (f32[8,4,4096]{2,1,0:T(4,128)S(1)}, f32[8,4,4096]{2,1,0:T(4,128)}, u32[]{:S(2)}) copy-start(f32[8,4,4096]{2,1,0:T(4,128)} %param.7) | copy-start | bytes 1572868
  3.0 14.9 %copy-start.6 = (s32[8,4]{0,1:T(4,128)S(1)}, s32[8,4]{0,1:T(4,128)}, u32[]{:S(2)}) copy-start(s32[8,4]{0,1:T(4,128)} %param.11) | copy-start | bytes 388
  3.0 38.4 %all-to-all-start = ((f32[8,8,2,4,4,128]{5,3,4,1,2,0:T(4,128)}), f32[8,8,2,4,4,128]{5,3,4,1,2,0:T(4,128)}, u32[]{:S(2)}, u32[]{:S(2)}) async-start(f32[8,8,2,4,4,128]{5,3,4,1,2,0:T(4,128)} %broadcast_in_dim.8), calls=%async_computation | async-start | bytes 2097152 | tf_op jit(solution)/shard_map/all_to_all | solution.py:143
  12.1 7.7 %copy-start.7 = (s32[8,4]{0,1:T(4,128)S(1)}, s32[8,4]{0,1:T(4,128)}, u32[]{:S(2)}) copy-start(s32[8,4]{0,1:T(4,128)} %param.12) | copy-start | bytes 388
  13.2 51.3 %collective-permute-start = (f32[32,8,1,128]{3,0,2,1:T(8,128)}, f32[32,8,1,128]{3,0,2,1:T(8,128)S(1)}, u32[]{:S(2)}, u32[]{:S(2)}) collective-permute-start(f32[32,8,1,128]{3,0,2,1:T(8,128)} %get-tuple-element.6), channel_id=1, source_target_pairs={{0,32},{32,64},{64,96},{96,128},{128,160},{160,192},{192,224},{1,3... | collective-permute-start | bytes 393224 | tf_op jit(solution)/shard_map/ppermute | solution.py:28
  16.5 47.9 %collective-permute-start.1 = (f32[32,8,1,128]{3,0,2,1:T(8,128)}, f32[32,8,1,128]{3,0,2,1:T(8,128)}, u32[]{:S(2)}, u32[]{:S(2)}) collective-permute-start(f32[32,8,1,128]{3,0,2,1:T(8,128)} %get-tuple-element.7), channel_id=1, source_target_pairs={{32,0},{64,32},{96,64},{128,96},{160,128},{192,160},{224,192},{33,... | collective-permute-start | bytes 393224 | tf_op jit(solution)/shard_map/ppermute | solution.py:31
  41.4 23.1 %all-to-all-start.1 = ((f32[32,8,4,128]{3,2,1,0:T(4,128)}), f32[32,8,4,128]{3,2,1,0:T(4,128)S(1)}, u32[]{:S(2)}, u32[]{:S(2)}) async-start(f32[32,8,4,128]{3,2,1,0:T(4,128)} %bitcast.38), calls=%async_computation.1 | async-start | bytes 1048576 | tf_op jit(solution)/shard_map/all_to_all | solution.py:220
  67.5 20.8 %copy-start.5 = (bf16[4,128,128]{2,1,0:T(8,128)(2,1)S(1)}, bf16[4,128,128]{2,1,0:T(8,128)(2,1)}, u32[]{:S(2)}) copy-start(bf16[4,128,128]{2,1,0:T(8,128)(2,1)} %param.9) | copy-start | bytes 393220
  89.9 20.4 %copy-start.2 = (f32[8,4,32,128]{3,2,1,0:T(8,128)S(1)}, f32[8,4,32,128]{3,2,1,0:T(8,128)}, u32[]{:S(2)}) copy-start(f32[8,4,32,128]{3,2,1,0:T(8,128)} %get-tuple-element.3) | copy-start | bytes 1572868
  105.9 14.1 %all-to-all-start.4 = ((f32[32,8,384]{2,1,0:T(8,128)}), f32[32,8,384]{2,1,0:T(8,128)S(1)}, u32[]{:S(2)}, u32[]{:S(2)}) async-start(f32[32,8,384]{2,1,0:T(8,128)} %broadcast_in_dim.10), calls=%async_computation.4 | async-start | bytes 786432 | tf_op jit(solution)/shard_map/all_to_all | solution.py:137
  138.5 5.2 %copy-start.4 = (f32[128,128]{1,0:T(8,128)S(1)}, f32[128,128]{1,0:T(8,128)}, u32[]{:S(2)}) copy-start(f32[128,128]{1,0:T(8,128)} %fusion.95) | copy-start | bytes 196612
  146.1 3.2 %copy-start.1 = (f32[128,256]{1,0:T(8,128)S(1)}, f32[128,256]{1,0:T(8,128)}, u32[]{:S(2)}) copy-start(f32[128,256]{1,0:T(8,128)} %shard_map.86) | copy-start | bytes 393220

commit v7 on v6

--- a/solution.py
+++ b/solution.py
@@ -191,15 +191,15 @@
     s_im = (matmul_hi(yt_im, f_cos) - matmul_hi(yt_re, f_sin)) * row_scale
     s_re = s_re.reshape(chan_count, tiles_n, row_count, block)
     s_im = s_im.reshape(chan_count, tiles_n, row_count, block)
-    z_re = jnp.einsum("ctrj,ctjm->ctrm", s_re, grid_tiles, precision=HI)
-    z_im = jnp.einsum("ctrj,ctjm->ctrm", s_im, grid_tiles, precision=HI)
+    z_re = jnp.einsum("ctrj,ctjm->ctrm", s_re, grid_tiles, precision=lax.Precision.HIGH)
+    z_im = jnp.einsum("ctrj,ctjm->ctrm", s_im, grid_tiles, precision=lax.Precision.HIGH)
     place = jax.nn.one_hot(vis_block, vb_n, dtype=jnp.float32)
     r_re = jnp.einsum("ctv,ctrm->cvrm", place, z_re, precision=HI) - u_re
     r_im = jnp.einsum("ctv,ctrm->cvrm", place, z_im, precision=HI) - u_im
     sp_re = jnp.einsum("ctv,cvrm->ctrm", place, r_re, precision=HI)
     sp_im = jnp.einsum("ctv,cvrm->ctrm", place, r_im, precision=HI)
-    c_re = jnp.einsum("ctrm,ctjm->ctrj", sp_re, grid_tiles, precision=HI)
-    c_im = jnp.einsum("ctrm,ctjm->ctrj", sp_im, grid_tiles, precision=HI)
+    c_re = jnp.einsum("ctrm,ctjm->ctrj", sp_re, grid_tiles, precision=lax.Precision.HIGH)
+    c_im = jnp.einsum("ctrm,ctjm->ctrj", sp_im, grid_tiles, precision=lax.Precision.HIGH)
     c_re = c_re.reshape(flat, block)
     c_im = c_im.reshape(flat, block)
     d_re = (matmul_hi(c_re, f_cos) - matmul_hi(c_im, f_sin)) * row_scale

time: 155 us -> 151 us (0.974)
  matrix products: 45.8 us -> 40.7 us
  waiting for transfers between devices: 24.4 us -> 26.1 us
    dot_general x4, matrix products: 10.4 us -> 5.28 us  [the longest x1 1.72 us: data_gradient(): jnp.einsum('ctrm,ctjm->ctrj', sp_im, grid_tiles, precision=lax.Precision....]
    all_to_all x1, waiting for transfers between devices: 15.7 us -> 17.6 us  [exchange_gather(): return lax.all_to_all(spread, axis, 0, 0, tiled=True)]
  transfers between devices with their start and end apart: 5 -> 5, of which waited for: 2 -> 2; matrix products, arithmetic and copies ran while one was open for 17% -> 14% of each run, Pallas kernels for 0% -> 0%
where the time goes in v7:
time: 151 us
  matrix products  40.7 us (27%)
  blocking collectives  32.8 us (22%)
  waiting for transfers between devices  26.1 us (17%)
  starting transfers between devices  25.3 us (17%)
  Pallas kernels  10.8 us (7%)
  local copies, waits for them, and re-layouts  9.64 us (6%)
  between operations  3.57 us (2%)
  other arithmetic  1.69 us (1%)
    all_to_all x1, blocking collectives, _on_device(): lax.all_to_all(rest, 'chan', 0, 0, tiled=True).reshape(dual_field.shape)  18.6 us
    all_to_all x1, waiting for transfers between devices, exchange_gather(): return lax.all_to_all(spread, axis, 0, 0, tiled=True)  17.6 us
    all_to_all x1, blocking collectives, exchange_sum(): mine = jnp.sum(lax.all_to_all(pieces, axis, 0, 0, tiled=True), axis=0)  14.2 us
    dot_general x17, matrix products, matmul_hi(): return jnp.dot(first_mat, second_mat, precision=HI)  13.8 us
    pallas_call x1, Pallas kernels, basis_transposed(): pl.pallas_call(_basis_kernel, out_shape=jax.ShapeDtypeStruct(side.shape,...  10.8 us
    dot_general x52, matrix products, iter_mm(): return jnp.dot(first_mat, second_mat, precision=lax.Precision.HIGH)  9.53 us
    all_to_all x1, starting transfers between devices, exchange_gather(): return lax.all_to_all(spread, axis, 0, 0, tiled=True)  9.13 us
    all_to_all x1, waiting for transfers between devices, exchange_sum(): return lax.all_to_all(spread, axis, 0, 0, tiled=True).reshape(value.shape)  8.58 us
  transfers between devices with their start and end apart: 5, of which 2 were waited for; matrix products, arithmetic and copies ran while one was open for 14% of the time, Pallas kernels for 0%

profile of v7, /device:TPU:1, one launch (start us, length us, event | category | flops | bytes accessed | tf_op | source)
XLA Modules:
  0.0 150.6 jit_solution(717917406291723450)
XLA Ops:
  0.7 1.1 copy.102
  1.8 1.2 broadcast_in_dim.8
  3.0 9.1 %all-to-all-start = ((f32[8,8,2,4,4,128]{5,3,4,1,2,0:T(4,128)}), f32[8,8,2,4,4,128]{5,3,4,1,2,0:T(4,128)}, u32[]{:S(2)}, u32[]{:S(2)}) async-start(f32[8,8,2,4,4,128]{5,3,4,1,2,0:T(4,128)} %broadcast_in_dim.8), calls=%async_computation | async-start | bytes 2097152 | tf_op jit(solution)/shard_map/all_to_all | solution.py:143
  12.1 0.4 reshape.78
  12.5 0.7 fusion.250
  13.2 3.3 %collective-permute-start = (f32[32,8,1,128]{3,0,2,1:T(8,128)}, f32[32,8,1,128]{3,0,2,1:T(8,128)S(1)}, u32[]{:S(2)}, u32[]{:S(2)}) collective-permute-start(f32[32,8,1,128]{3,0,2,1:T(8,128)} %get-tuple-element.6), channel_id=1, source_target_pairs={{0,32},{32,64},{64,96},{96,128},{128,160},{160,192},{192,224},{1,3... | collective-permute-start | bytes 393224 | tf_op jit(solution)/shard_map/ppermute | solution.py:28
  16.5 1.3 collective-permute-start.1
  17.9 0.2 fusion.158
  18.2 0.6 convolution_negate_fusion
  18.7 0.6 multiply_subtract_fusion.1
  19.3 0.5 fusion.120
  19.9 0.5 fusion.124
  20.4 0.5 fusion.32
  20.8 0.9 fusion.256
  21.8 0.3 fusion.83
  22.1 0.5 fusion.33
  22.6 0.9 fusion.255
  23.5 0.3 fusion.90
  23.8 17.6 %all-to-all-done = f32[8,8,2,4,4,128]{5,3,4,1,2,0:T(4,128)} async-done(((f32[8,8,2,4,4,128]{5,3,4,1,2,0:T(4,128)}), f32[8,8,2,4,4,128]{5,3,4,1,2,0:T(4,128)}, u32[]{:S(2)}, u32[]{:S(2)}) %all-to-all-start) | async-done | bytes 1048608 | tf_op jit(solution)/shard_map/all_to_all | solution.py:143
  41.4 7.7 %all-to-all-start.1 = ((f32[32,8,4,128]{3,2,1,0:T(4,128)}), f32[32,8,4,128]{3,2,1,0:T(4,128)S(1)}, u32[]{:S(2)}, u32[]{:S(2)}) async-start(f32[32,8,4,128]{3,2,1,0:T(4,128)} %bitcast.38), calls=%async_computation.1 | async-start | bytes 1048576 | tf_op jit(solution)/shard_map/all_to_all | solution.py:220
  49.1 1.3 fusion.249
  50.4 0.8 convolution_bitcast_fusion.2
  51.2 0.8 convolution_bitcast_fusion.4
  52.0 0.8 convolution_bitcast_fusion.3
  52.8 0.8 convolution_bitcast_fusion.5
  53.7 0.3 fusion.80
  54.0 1.7 %fusion.78 = f32[8,4,4,128]{3,2,1,0:T(4,128)S(1)} fusion(f32[8,4,128,128]{3,2,1,0:T(8,128)S(1)} %copy-done, f32[8,4,4,128]{3,1,2,0:T(4,128)S(1)} %fusion.80), kind=kOutput, calls=%fused_computation.135 | convolution fusion | flops 12582912 | bytes 2228224 | tf_op jit(solution)/shard_map/ctrm,ctjm->ctrj/dot_general | solution.py:202
  55.8 0.3 fusion.87
  56.0 1.7 %fusion.85 = f32[8,4,4,128]{3,2,1,0:T(4,128)S(1)} fusion(f32[8,4,128,128]{3,2,1,0:T(8,128)S(1)} %copy-done, f32[8,4,4,128]{3,1,2,0:T(4,128)S(1)} %fusion.87), kind=kOutput, calls=%fused_computation.143 | convolution fusion | flops 12582912 | bytes 2228224 | tf_op jit(solution)/shard_map/ctrm,ctjm->ctrj/dot_general | solution.py:201
  57.8 0.5 fusion.122
  58.2 0.5 fusion.31
  58.7 0.5 fusion.126
  59.2 0.5 fusion.30
  59.6 1.6 %fusion.100 = f32[8,4,128,32]{2,3,1,0:T(8,128)} fusion(f32[8,4,4,128]{3,2,1,0:T(4,128)S(1)} %bitcast.223, f32[8,4,4,128]{3,2,1,0:T(4,128)S(1)} %bitcast.221, f32[8,4,128]{2,1,0:T(4,128)S(1)} %get-tuple-element.11, f32[8,4,128]{2,1,0:T(4,128)S(1)} %get-tuple-element.10, s32[8,4]{1,0:T(8,128)S(1)} %copy.96), kind=kOutput, calls=%fused_computation.163 | convolution fusion | flops 6354944 | bytes 688256 | tf_op jit(solution)/shard_map/ctn,ctrm->ncrm/dot_general | solution.py:211
  61.2 3.1 %multiply_subtract_fusion = (f32[32,8,4,128]{3,0,2,1:T(8,128)S(1)}, f32[8,4,32,128]{3,2,1,0:T(8,128)}) fusion(f32[32,8,4,128]{3,0,2,1:T(8,128)S(1)} %bitcast.215, f32[32,8,1,128]{3,0,2,1:T(8,128)} %collective-permute-done.1, f32[32,8,1,128]{3,0,2,1:T(8,128)S(1)} %collective-permute-done, f32[32,8,4,128]{3,2,1,0:T(4,128)S(1)} %all-to-all-done.1, ...), kind=kOutput, calls=%fused_computation.91 | convolution fusion | flops 8189952 | bytes 3047552 | tf_op jit(solution)/shard_map/ctn,ctrm->ncrm/dot_general | solution.py:211
  64.3 0.3 copy.125
  64.6 18.6 %all_to_all.25 = f32[32,8,4,128]{3,2,1,0:T(4,128)S(1)} all-to-all(f32[32,8,4,128]{3,2,1,0:T(4,128)S(1)} %copy.125), channel_id=1, replica_groups=mesh['facet'=8,'chan'=32] {'chan'}, dimensions={0} | all-to-all | bytes 1048576 | tf_op jit(solution)/shard_map/all_to_all | solution.py:233
  83.2 1.9 %convolution_bitcast_fusion = f32[256,256]{0,1:T(8,128)S(1)} fusion(f32[32,8,4,128]{3,2,1,0:T(4,128)S(1)} %all_to_all.25, f32[256,4,128]{2,1,0:T(4,128)} %param.8), kind=kOutput, calls=%fused_computation.3 | convolution fusion | flops 402915328 | bytes 1310720 | tf_op jit(solution)/shard_map/dot_general | solution.py:240
  85.1 1.5 %convolution_bitcast_fusion.1 = f32[256,128]{0,1:T(8,128)S(1)} fusion(bf16[4,128,128]{2,1,0:T(8,128)(2,1)S(1)} %copy-done.5, f32[32,8,4,128]{3,2,1,0:T(4,128)S(1)} %all_to_all.25, f32[256,4,128]{2,1,0:T(4,128)} %param.8), kind=kOutput, calls=%fused_computation.4 | convolution fusion | flops 201588736 | bytes 1310720 | tf_op jit(solution)/shard_map/dot_general | solution.py:37
  86.7 0.9 copy.129
  87.6 14.2 %all_to_all.26 = f32[32,8,384]{2,1,0:T(8,128)S(1)} all-to-all(f32[32,8,384]{2,1,0:T(8,128)} %bitcast.219), channel_id=1, replica_groups=mesh['facet'=8,'chan'=32] {'chan'}, dimensions={0} | all-to-all | bytes 786432 | tf_op jit(solution)/shard_map/all_to_all | solution.py:135
  101.8 0.8 broadcast_in_dim.10
  102.6 3.9 %all-to-all-start.4 = ((f32[32,8,384]{2,1,0:T(8,128)}), f32[32,8,384]{2,1,0:T(8,128)S(1)}, u32[]{:S(2)}, u32[]{:S(2)}) async-start(f32[32,8,384]{2,1,0:T(8,128)} %broadcast_in_dim.10), calls=%async_computation.4 | async-start | bytes 786432 | tf_op jit(solution)/shard_map/all_to_all | solution.py:137
  106.5 0.6 fusion.95
  107.1 1.0 reshape.88
  108.1 8.6 %all-to-all-done.4 = f32[32,8,384]{2,1,0:T(8,128)S(1)} async-done(((f32[32,8,384]{2,1,0:T(8,128)}), f32[32,8,384]{2,1,0:T(8,128)S(1)}, u32[]{:S(2)}, u32[]{:S(2)}) %all-to-all-start.4) | async-done | bytes 393248 | tf_op jit(solution)/shard_map/all_to_all | solution.py:137
  116.7 1.0 fusion.242.gram_ref
  117.7 0.8 copy.150
  118.5 10.8 %shard_map.86 = f32[128,256]{1,0:T(8,128)} custom-call(f32[128,128]{1,0:T(8,128)} %fusion.242.gram_ref, f32[128,256]{1,0:T(8,128)} %bitcast.220), custom_call_target="tpu_custom_call" | custom-call | flops 25165824 | bytes 327680 | tf_op jit(solution)/shard_map/pallas_call | solution.py:109
  129.2 1.3 fusion.44
  130.5 1.8 %select_reduce_fusion = (f32[]{:T(128)}, f32[128,128]{1,0:T(8,128)S(1)}) fusion(f32[128,256]{1,0:T(8,128)} %shard_map.86, f32[256,128]{1,0:T(8,128)S(1)} %fusion.44), kind=kOutput, calls=%fused_computation.156 | convolution fusion | flops 50380800 | bytes 327684 | tf_op jit(solution)/shard_map/dot_general | solution.py:37
  133.0 0.6 multiply_reduce_fusion.1
  138.8 0.8 multiply_reduce_fusion
  140.5 0.2 fusion.46
  140.9 0.2 fusion.268
  141.3 0.2 fusion.269
  141.7 0.2 fusion.270
  142.1 0.2 fusion.271
  142.5 0.2 fusion.272
  145.8 0.2 fusion.92
  146.1 0.4 fusion.280
  146.4 1.5 %fusion.34 = f32[128,512]{1,0:T(8,128)S(1)} fusion(f32[128,256]{1,0:T(8,128)S(1)} %copy-done.1, f32[32,8,4,128]{3,2,1,0:T(4,128)S(1)} %all_to_all.25, f32[256,4,128]{2,1,0:T(4,128)} %param.8), kind=kOutput, calls=%fused_computation.75 | convolution fusion | flops 201588736 | bytes 1441792 | tf_op jit(solution)/shard_map/dot_general | solution.py:37
  148.0 1.6 %convolution_subtract_fusion.1 = f32[256,512]{1,0:T(8,128)S(1)} fusion(f32[256,128]{1,0:T(8,128)S(1)} %fusion.280, f32[128,512]{1,0:T(8,128)S(1)} %fusion.34, f32[32,8,4,128]{3,2,1,0:T(4,128)S(1)} %all_to_all.25, f32[256,4,128]{2,1,0:T(4,128)} %param.8), kind=kOutput, calls=%fused_computation.2 | convolution fusion | flops 201719808 | bytes 1966080 | tf_op jit(solution)/shard_map/dot_general | solution.py:37
  149.6 1.0 reshape.93
  (77 shorter events, 8.8 us)
Async XLA Ops:
  0.6 20.2 %copy-start = (f32[8,4,128,128]{3,2,1,0:T(8,128)S(1)}, f32[8,4,128,128]{3,2,1,0:T(8,128)}, u32[]{:S(2)}) copy-start(f32[8,4,128,128]{3,2,1,0:T(8,128)} %param.10) | copy-start | bytes 6291460
  0.6 11.5 %copy-start.3 = (f32[8,4,4096]{2,1,0:T(4,128)S(1)}, f32[8,4,4096]{2,1,0:T(4,128)}, u32[]{:S(2)}) copy-start(f32[8,4,4096]{2,1,0:T(4,128)} %param.7) | copy-start | bytes 1572868
  3.0 14.9 %copy-start.6 = (s32[8,4]{0,1:T(4,128)S(1)}, s32[8,4]{0,1:T(4,128)}, u32[]{:S(2)}) copy-start(s32[8,4]{0,1:T(4,128)} %param.11) | copy-start | bytes 388
  3.0 38.4 %all-to-all-start = ((f32[8,8,2,4,4,128]{5,3,4,1,2,0:T(4,128)}), f32[8,8,2,4,4,128]{5,3,4,1,2,0:T(4,128)}, u32[]{:S(2)}, u32[]{:S(2)}) async-start(f32[8,8,2,4,4,128]{5,3,4,1,2,0:T(4,128)} %broadcast_in_dim.8), calls=%async_computation | async-start | bytes 2097152 | tf_op jit(solution)/shard_map/all_to_all | solution.py:143
  12.1 7.7 %copy-start.7 = (s32[8,4]{0,1:T(4,128)S(1)}, s32[8,4]{0,1:T(4,128)}, u32[]{:S(2)}) copy-start(s32[8,4]{0,1:T(4,128)} %param.12) | copy-start | bytes 388
  13.2 48.0 %collective-permute-start = (f32[32,8,1,128]{3,0,2,1:T(8,128)}, f32[32,8,1,128]{3,0,2,1:T(8,128)S(1)}, u32[]{:S(2)}, u32[]{:S(2)}) collective-permute-start(f32[32,8,1,128]{3,0,2,1:T(8,128)} %get-tuple-element.6), channel_id=1, source_target_pairs={{0,32},{32,64},{64,96},{96,128},{128,160},{160,192},{192,224},{1,3... | collective-permute-start | bytes 393224 | tf_op jit(solution)/shard_map/ppermute | solution.py:28
  16.5 44.6 %collective-permute-start.1 = (f32[32,8,1,128]{3,0,2,1:T(8,128)}, f32[32,8,1,128]{3,0,2,1:T(8,128)}, u32[]{:S(2)}, u32[]{:S(2)}) collective-permute-start(f32[32,8,1,128]{3,0,2,1:T(8,128)} %get-tuple-element.7), channel_id=1, source_target_pairs={{32,0},{64,32},{96,64},{128,96},{160,128},{192,160},{224,192},{33,... | collective-permute-start | bytes 393224 | tf_op jit(solution)/shard_map/ppermute | solution.py:31
  41.4 19.8 %all-to-all-start.1 = ((f32[32,8,4,128]{3,2,1,0:T(4,128)}), f32[32,8,4,128]{3,2,1,0:T(4,128)S(1)}, u32[]{:S(2)}, u32[]{:S(2)}) async-start(f32[32,8,4,128]{3,2,1,0:T(4,128)} %bitcast.38), calls=%async_computation.1 | async-start | bytes 1048576 | tf_op jit(solution)/shard_map/all_to_all | solution.py:220
  64.3 20.8 %copy-start.5 = (bf16[4,128,128]{2,1,0:T(8,128)(2,1)S(1)}, bf16[4,128,128]{2,1,0:T(8,128)(2,1)}, u32[]{:S(2)}) copy-start(bf16[4,128,128]{2,1,0:T(8,128)(2,1)} %param.9) | copy-start | bytes 393220
  86.7 20.5 %copy-start.2 = (f32[8,4,32,128]{3,2,1,0:T(8,128)S(1)}, f32[8,4,32,128]{3,2,1,0:T(8,128)}, u32[]{:S(2)}) copy-start(f32[8,4,32,128]{3,2,1,0:T(8,128)} %get-tuple-element.3) | copy-start | bytes 1572868
  102.6 14.1 %all-to-all-start.4 = ((f32[32,8,384]{2,1,0:T(8,128)}), f32[32,8,384]{2,1,0:T(8,128)S(1)}, u32[]{:S(2)}, u32[]{:S(2)}) async-start(f32[32,8,384]{2,1,0:T(8,128)} %broadcast_in_dim.10), calls=%async_computation.4 | async-start | bytes 786432 | tf_op jit(solution)/shard_map/all_to_all | solution.py:137
  135.2 5.2 %copy-start.4 = (f32[128,128]{1,0:T(8,128)S(1)}, f32[128,128]{1,0:T(8,128)}, u32[]{:S(2)}) copy-start(f32[128,128]{1,0:T(8,128)} %fusion.95) | copy-start | bytes 196612
  142.9 3.2 %copy-start.1 = (f32[128,256]{1,0:T(8,128)S(1)}, f32[128,256]{1,0:T(8,128)}, u32[]{:S(2)}) copy-start(f32[128,256]{1,0:T(8,128)} %shard_map.86) | copy-start | bytes 393220

commit v8 on v7

--- a/solution.py
+++ b/solution.py
@@ -35,6 +35,10 @@
 
 def matmul_hi(first_mat, second_mat):
     return jnp.dot(first_mat, second_mat, precision=HI)
+
+
+def matmul_lo(first_mat, second_mat):
+    return jnp.dot(first_mat, second_mat, precision=lax.Precision.HIGH)
 
 
 def shrink_matrix(gram_mat):
@@ -179,36 +183,36 @@
     f_cos, f_sin = phase_of(j_idx * m_idx, block)
     row_scale = 1.0 / math.sqrt(width)
 
-    y_re = jnp.einsum("ctn,ncrm->ctrm", w_cos, sky_b, precision=HI)
-    y_im = -jnp.einsum("ctn,ncrm->ctrm", w_sin, sky_b, precision=HI)
+    y_re = jnp.einsum("ctn,ncrm->ctrm", w_cos, sky_b, precision=lax.Precision.HIGH)
+    y_im = -jnp.einsum("ctn,ncrm->ctrm", w_sin, sky_b, precision=lax.Precision.HIGH)
     yt_re = y_re * t_cos + y_im * t_sin
     yt_im = y_im * t_cos - y_re * t_sin
     tiles_n = freq_block.shape[1]
     flat = chan_count * tiles_n * row_count
     yt_re = yt_re.reshape(flat, block)
     yt_im = yt_im.reshape(flat, block)
-    s_re = (matmul_hi(yt_re, f_cos) + matmul_hi(yt_im, f_sin)) * row_scale
-    s_im = (matmul_hi(yt_im, f_cos) - matmul_hi(yt_re, f_sin)) * row_scale
+    s_re = (matmul_lo(yt_re, f_cos) + matmul_lo(yt_im, f_sin)) * row_scale
+    s_im = (matmul_lo(yt_im, f_cos) - matmul_lo(yt_re, f_sin)) * row_scale
     s_re = s_re.reshape(chan_count, tiles_n, row_count, block)
     s_im = s_im.reshape(chan_count, tiles_n, row_count, block)
     z_re = jnp.einsum("ctrj,ctjm->ctrm", s_re, grid_tiles, precision=lax.Precision.HIGH)
     z_im = jnp.einsum("ctrj,ctjm->ctrm", s_im, grid_tiles, precision=lax.Precision.HIGH)
     place = jax.nn.one_hot(vis_block, vb_n, dtype=jnp.float32)
-    r_re = jnp.einsum("ctv,ctrm->cvrm", place, z_re, precision=HI) - u_re
-    r_im = jnp.einsum("ctv,ctrm->cvrm", place, z_im, precision=HI) - u_im
-    sp_re = jnp.einsum("ctv,cvrm->ctrm", place, r_re, precision=HI)
-    sp_im = jnp.einsum("ctv,cvrm->ctrm", place, r_im, precision=HI)
+    r_re = jnp.einsum("ctv,ctrm->cvrm", place, z_re, precision=lax.Precision.HIGH) - u_re
+    r_im = jnp.einsum("ctv,ctrm->cvrm", place, z_im, precision=lax.Precision.HIGH) - u_im
+    sp_re = jnp.einsum("ctv,cvrm->ctrm", place, r_re, precision=lax.Precision.HIGH)
+    sp_im = jnp.einsum("ctv,cvrm->ctrm", place, r_im, precision=lax.Precision.HIGH)
     c_re = jnp.einsum("ctrm,ctjm->ctrj", sp_re, grid_tiles, precision=lax.Precision.HIGH)
     c_im = jnp.einsum("ctrm,ctjm->ctrj", sp_im, grid_tiles, precision=lax.Precision.HIGH)
     c_re = c_re.reshape(flat, block)
     c_im = c_im.reshape(flat, block)
-    d_re = (matmul_hi(c_re, f_cos) - matmul_hi(c_im, f_sin)) * row_scale
-    d_im = (matmul_hi(c_re, f_sin) + matmul_hi(c_im, f_cos)) * row_scale
+    d_re = (matmul_lo(c_re, f_cos) - matmul_lo(c_im, f_sin)) * row_scale
+    d_im = (matmul_lo(c_re, f_sin) + matmul_lo(c_im, f_cos)) * row_scale
     d_re = d_re.reshape(chan_count, tiles_n, row_count, block)
     d_im = d_im.reshape(chan_count, tiles_n, row_count, block)
     dt_re = d_re * t_cos - d_im * t_sin
     dt_im = d_im * t_cos + d_re * t_sin
-    return jnp.einsum("ctn,ctrm->ncrm", w_cos, dt_re, precision=HI) - jnp.einsum(
+    return jnp.einsum("ctn,ctrm->ncrm", w_cos, dt_re, precision=lax.Precision.HIGH) - jnp.einsum(
         "ctn,ctrm->ncrm", w_sin, dt_im, precision=HI
     )
 

time: 151 us -> 151 us (level)
    dot_general x17 -> x9, matrix products: 13.8 us -> 10.2 us  [matmul_hi(): return jnp.dot(first_mat, second_mat, precision=HI)]
    dot_general x7 -> x15, matrix products: 3.85 us -> 6.67 us  [the longest x8 3.41 us: matmul_lo(): return jnp.dot(first_mat, second_mat, precision=lax.Precision.HIGH)]
  transfers between devices with their start and end apart: 5 -> 5, of which waited for: 2 -> 2; matrix products, arithmetic and copies ran while one was open for 14% -> 13% of each run, Pallas kernels for 0% -> 0%
where the time goes in v8:
time: 151 us; the launch traced here: 150 us
  matrix products  39.8 us (26%)
  blocking collectives  32.8 us (22%)
  waiting for transfers between devices  26.6 us (18%)
  starting transfers between devices  25.3 us (17%)
  Pallas kernels  10.8 us (7%)
  local copies, waits for them, and re-layouts  9.64 us (6%)
  between operations  3.57 us (2%)
  other arithmetic  1.69 us (1%)
    all_to_all x1, blocking collectives, _on_device(): lax.all_to_all(rest, 'chan', 0, 0, tiled=True).reshape(dual_field.shape)  18.6 us
    all_to_all x1, waiting for transfers between devices, exchange_gather(): return lax.all_to_all(spread, axis, 0, 0, tiled=True)  18 us
    all_to_all x1, blocking collectives, exchange_sum(): mine = jnp.sum(lax.all_to_all(pieces, axis, 0, 0, tiled=True), axis=0)  14.2 us
    pallas_call x1, Pallas kernels, basis_transposed(): pl.pallas_call(_basis_kernel, out_shape=jax.ShapeDtypeStruct(side.shape,...  10.8 us
    dot_general x9, matrix products, matmul_hi(): return jnp.dot(first_mat, second_mat, precision=HI)  10.2 us
    dot_general x52, matrix products, iter_mm(): return jnp.dot(first_mat, second_mat, precision=lax.Precision.HIGH)  9.53 us
    all_to_all x1, starting transfers between devices, exchange_gather(): return lax.all_to_all(spread, axis, 0, 0, tiled=True)  9.13 us
    all_to_all x1, waiting for transfers between devices, exchange_sum(): return lax.all_to_all(spread, axis, 0, 0, tiled=True).reshape(value.shape)  8.58 us
  transfers between devices with their start and end apart: 5, of which 2 were waited for; matrix products, arithmetic and copies ran while one was open for 13% of the time, Pallas kernels for 0%

profile of v8, /device:TPU:1, one launch (start us, length us, event | category | flops | bytes accessed | tf_op | source)
XLA Modules:
  0.0 150.2 jit_solution(12453294108302644783)
XLA Ops:
  0.7 1.1 copy.102
  1.8 1.2 broadcast_in_dim.8
  3.0 9.1 %all-to-all-start = ((f32[8,8,2,4,4,128]{5,3,4,1,2,0:T(4,128)}), f32[8,8,2,4,4,128]{5,3,4,1,2,0:T(4,128)}, u32[]{:S(2)}, u32[]{:S(2)}) async-start(f32[8,8,2,4,4,128]{5,3,4,1,2,0:T(4,128)} %broadcast_in_dim.8), calls=%async_computation | async-start | bytes 2097152 | tf_op jit(solution)/shard_map/all_to_all | solution.py:147
  12.1 0.4 reshape.78
  12.5 0.7 fusion.250
  13.2 3.3 %collective-permute-start = (f32[32,8,1,128]{3,0,2,1:T(8,128)}, f32[32,8,1,128]{3,0,2,1:T(8,128)S(1)}, u32[]{:S(2)}, u32[]{:S(2)}) collective-permute-start(f32[32,8,1,128]{3,0,2,1:T(8,128)} %get-tuple-element.6), channel_id=1, source_target_pairs={{0,32},{32,64},{64,96},{96,128},{128,160},{160,192},{192,224},{1,3... | collective-permute-start | bytes 393224 | tf_op jit(solution)/shard_map/ppermute | solution.py:28
  16.5 1.3 collective-permute-start.1
  17.9 0.2 fusion.158
  18.2 0.4 convolution_negate_fusion
  18.6 0.4 multiply_subtract_fusion.1
  19.1 0.4 fusion.120
  19.6 0.4 fusion.124
  20.0 0.4 fusion.32
  20.5 0.9 fusion.256
  21.4 0.3 fusion.83
  21.7 0.4 fusion.33
  22.2 0.9 fusion.255
  23.1 0.3 fusion.90
  23.4 18.0 %all-to-all-done = f32[8,8,2,4,4,128]{5,3,4,1,2,0:T(4,128)} async-done(((f32[8,8,2,4,4,128]{5,3,4,1,2,0:T(4,128)}), f32[8,8,2,4,4,128]{5,3,4,1,2,0:T(4,128)}, u32[]{:S(2)}, u32[]{:S(2)}) %all-to-all-start) | async-done | bytes 1048608 | tf_op jit(solution)/shard_map/all_to_all | solution.py:147
  41.4 7.7 %all-to-all-start.1 = ((f32[32,8,4,128]{3,2,1,0:T(4,128)}), f32[32,8,4,128]{3,2,1,0:T(4,128)S(1)}, u32[]{:S(2)}, u32[]{:S(2)}) async-start(f32[32,8,4,128]{3,2,1,0:T(4,128)} %bitcast.38), calls=%async_computation.1 | async-start | bytes 1048576 | tf_op jit(solution)/shard_map/all_to_all | solution.py:224
  49.1 1.3 fusion.249
  50.4 0.8 convolution_bitcast_fusion.2
  51.2 0.8 convolution_bitcast_fusion.4
  52.0 0.8 convolution_bitcast_fusion.3
  52.8 0.8 convolution_bitcast_fusion.5
  53.7 0.2 fusion.80
  53.9 1.7 %fusion.78 = f32[8,4,4,128]{3,2,1,0:T(4,128)S(1)} fusion(f32[8,4,128,128]{3,2,1,0:T(8,128)S(1)} %copy-done, f32[8,4,4,128]{3,1,2,0:T(4,128)S(1)} %fusion.80), kind=kOutput, calls=%fused_computation.135 | convolution fusion | flops 12582912 | bytes 2228224 | tf_op jit(solution)/shard_map/ctrm,ctjm->ctrj/dot_general | solution.py:206
  55.8 0.2 fusion.87
  56.0 1.7 %fusion.85 = f32[8,4,4,128]{3,2,1,0:T(4,128)S(1)} fusion(f32[8,4,128,128]{3,2,1,0:T(8,128)S(1)} %copy-done, f32[8,4,4,128]{3,1,2,0:T(4,128)S(1)} %fusion.87), kind=kOutput, calls=%fused_computation.143 | convolution fusion | flops 12582912 | bytes 2228224 | tf_op jit(solution)/shard_map/ctrm,ctjm->ctrj/dot_general | solution.py:205
  57.7 0.4 fusion.122
  58.2 0.4 fusion.31
  58.6 0.4 fusion.126
  59.0 0.4 fusion.30
  59.5 1.3 fusion.100
  60.8 3.1 %multiply_subtract_fusion = (f32[32,8,4,128]{3,0,2,1:T(8,128)S(1)}, f32[8,4,32,128]{3,2,1,0:T(8,128)}) fusion(f32[32,8,4,128]{3,0,2,1:T(8,128)S(1)} %bitcast.215, f32[32,8,1,128]{3,0,2,1:T(8,128)} %collective-permute-done.1, f32[32,8,1,128]{3,0,2,1:T(8,128)S(1)} %collective-permute-done, f32[32,8,4,128]{3,2,1,0:T(4,128)S(1)} %all-to-all-done.1, ...), kind=kOutput, calls=%fused_computation.91 | convolution fusion | flops 8189952 | bytes 3047552 | tf_op jit(solution)/shard_map/ctn,ctrm->ncrm/dot_general | solution.py:215
  63.9 0.3 copy.125
  64.2 18.6 %all_to_all.25 = f32[32,8,4,128]{3,2,1,0:T(4,128)S(1)} all-to-all(f32[32,8,4,128]{3,2,1,0:T(4,128)S(1)} %copy.125), channel_id=1, replica_groups=mesh['facet'=8,'chan'=32] {'chan'}, dimensions={0} | all-to-all | bytes 1048576 | tf_op jit(solution)/shard_map/all_to_all | solution.py:237
  82.8 1.9 %convolution_bitcast_fusion = f32[256,256]{0,1:T(8,128)S(1)} fusion(f32[32,8,4,128]{3,2,1,0:T(4,128)S(1)} %all_to_all.25, f32[256,4,128]{2,1,0:T(4,128)} %param.8), kind=kOutput, calls=%fused_computation.3 | convolution fusion | flops 402915328 | bytes 1310720 | tf_op jit(solution)/shard_map/dot_general | solution.py:244
  84.7 1.5 %convolution_bitcast_fusion.1 = f32[256,128]{0,1:T(8,128)S(1)} fusion(bf16[4,128,128]{2,1,0:T(8,128)(2,1)S(1)} %copy-done.5, f32[32,8,4,128]{3,2,1,0:T(4,128)S(1)} %all_to_all.25, f32[256,4,128]{2,1,0:T(4,128)} %param.8), kind=kOutput, calls=%fused_computation.4 | convolution fusion | flops 201588736 | bytes 1310720 | tf_op jit(solution)/shard_map/dot_general | solution.py:37
  86.3 0.9 copy.129
  87.2 14.2 %all_to_all.26 = f32[32,8,384]{2,1,0:T(8,128)S(1)} all-to-all(f32[32,8,384]{2,1,0:T(8,128)} %bitcast.219), channel_id=1, replica_groups=mesh['facet'=8,'chan'=32] {'chan'}, dimensions={0} | all-to-all | bytes 786432 | tf_op jit(solution)/shard_map/all_to_all | solution.py:139
  101.4 0.8 broadcast_in_dim.10
  102.2 3.9 %all-to-all-start.4 = ((f32[32,8,384]{2,1,0:T(8,128)}), f32[32,8,384]{2,1,0:T(8,128)S(1)}, u32[]{:S(2)}, u32[]{:S(2)}) async-start(f32[32,8,384]{2,1,0:T(8,128)} %broadcast_in_dim.10), calls=%async_computation.4 | async-start | bytes 786432 | tf_op jit(solution)/shard_map/all_to_all | solution.py:141
  106.1 0.6 fusion.95
  106.7 1.0 reshape.88
  107.7 8.6 %all-to-all-done.4 = f32[32,8,384]{2,1,0:T(8,128)S(1)} async-done(((f32[32,8,384]{2,1,0:T(8,128)}), f32[32,8,384]{2,1,0:T(8,128)S(1)}, u32[]{:S(2)}, u32[]{:S(2)}) %all-to-all-start.4) | async-done | bytes 393248 | tf_op jit(solution)/shard_map/all_to_all | solution.py:141
  116.3 1.0 fusion.242.gram_ref
  117.3 0.8 copy.150
  118.1 10.8 %shard_map.86 = f32[128,256]{1,0:T(8,128)} custom-call(f32[128,128]{1,0:T(8,128)} %fusion.242.gram_ref, f32[128,256]{1,0:T(8,128)} %bitcast.220), custom_call_target="tpu_custom_call" | custom-call | flops 25165824 | bytes 327680 | tf_op jit(solution)/shard_map/pallas_call | solution.py:113
  128.8 1.3 fusion.44
  130.1 1.8 %select_reduce_fusion = (f32[]{:T(128)}, f32[128,128]{1,0:T(8,128)S(1)}) fusion(f32[128,256]{1,0:T(8,128)} %shard_map.86, f32[256,128]{1,0:T(8,128)S(1)} %fusion.44), kind=kOutput, calls=%fused_computation.156 | convolution fusion | flops 50380800 | bytes 327684 | tf_op jit(solution)/shard_map/dot_general | solution.py:37
  132.6 0.6 multiply_reduce_fusion.1
  138.4 0.8 multiply_reduce_fusion
  140.1 0.2 fusion.46
  140.5 0.2 fusion.268
  140.9 0.2 fusion.269
  141.3 0.2 fusion.270
  142.1 0.2 fusion.272
  143.7 0.2 fusion.276
  145.4 0.2 fusion.92
  145.7 0.4 fusion.280
  146.1 1.5 %fusion.34 = f32[128,512]{1,0:T(8,128)S(1)} fusion(f32[128,256]{1,0:T(8,128)S(1)} %copy-done.1, f32[32,8,4,128]{3,2,1,0:T(4,128)S(1)} %all_to_all.25, f32[256,4,128]{2,1,0:T(4,128)} %param.8), kind=kOutput, calls=%fused_computation.75 | convolution fusion | flops 201588736 | bytes 1441792 | tf_op jit(solution)/shard_map/dot_general | solution.py:37
  147.6 1.6 %convolution_subtract_fusion.1 = f32[256,512]{1,0:T(8,128)S(1)} fusion(f32[256,128]{1,0:T(8,128)S(1)} %fusion.280, f32[128,512]{1,0:T(8,128)S(1)} %fusion.34, f32[32,8,4,128]{3,2,1,0:T(4,128)S(1)} %all_to_all.25, f32[256,4,128]{2,1,0:T(4,128)} %param.8), kind=kOutput, calls=%fused_computation.2 | convolution fusion | flops 201719808 | bytes 1966080 | tf_op jit(solution)/shard_map/dot_general | solution.py:37
  149.2 1.0 reshape.93
  (77 shorter events, 8.8 us)
Async XLA Ops:
  0.6 19.9 %copy-start = (f32[8,4,128,128]{3,2,1,0:T(8,128)S(1)}, f32[8,4,128,128]{3,2,1,0:T(8,128)}, u32[]{:S(2)}) copy-start(f32[8,4,128,128]{3,2,1,0:T(8,128)} %param.10) | copy-start | bytes 6291460
  0.6 11.5 %copy-start.3 = (f32[8,4,4096]{2,1,0:T(4,128)S(1)}, f32[8,4,4096]{2,1,0:T(4,128)}, u32[]{:S(2)}) copy-start(f32[8,4,4096]{2,1,0:T(4,128)} %param.7) | copy-start | bytes 1572868
  3.0 14.9 %copy-start.6 = (s32[8,4]{0,1:T(4,128)S(1)}, s32[8,4]{0,1:T(4,128)}, u32[]{:S(2)}) copy-start(s32[8,4]{0,1:T(4,128)} %param.11) | copy-start | bytes 388
  3.0 38.4 %all-to-all-start = ((f32[8,8,2,4,4,128]{5,3,4,1,2,0:T(4,128)}), f32[8,8,2,4,4,128]{5,3,4,1,2,0:T(4,128)}, u32[]{:S(2)}, u32[]{:S(2)}) async-start(f32[8,8,2,4,4,128]{5,3,4,1,2,0:T(4,128)} %broadcast_in_dim.8), calls=%async_computation | async-start | bytes 2097152 | tf_op jit(solution)/shard_map/all_to_all | solution.py:147
  12.1 7.4 %copy-start.7 = (s32[8,4]{0,1:T(4,128)S(1)}, s32[8,4]{0,1:T(4,128)}, u32[]{:S(2)}) copy-start(s32[8,4]{0,1:T(4,128)} %param.12) | copy-start | bytes 388
  13.2 47.6 %collective-permute-start = (f32[32,8,1,128]{3,0,2,1:T(8,128)}, f32[32,8,1,128]{3,0,2,1:T(8,128)S(1)}, u32[]{:S(2)}, u32[]{:S(2)}) collective-permute-start(f32[32,8,1,128]{3,0,2,1:T(8,128)} %get-tuple-element.6), channel_id=1, source_target_pairs={{0,32},{32,64},{64,96},{96,128},{128,160},{160,192},{192,224},{1,3... | collective-permute-start | bytes 393224 | tf_op jit(solution)/shard_map/ppermute | solution.py:28
  16.5 44.3 %collective-permute-start.1 = (f32[32,8,1,128]{3,0,2,1:T(8,128)}, f32[32,8,1,128]{3,0,2,1:T(8,128)}, u32[]{:S(2)}, u32[]{:S(2)}) collective-permute-start(f32[32,8,1,128]{3,0,2,1:T(8,128)} %get-tuple-element.7), channel_id=1, source_target_pairs={{32,0},{64,32},{96,64},{128,96},{160,128},{192,160},{224,192},{33,... | collective-permute-start | bytes 393224 | tf_op jit(solution)/shard_map/ppermute | solution.py:31
  41.4 19.4 %all-to-all-start.1 = ((f32[32,8,4,128]{3,2,1,0:T(4,128)}), f32[32,8,4,128]{3,2,1,0:T(4,128)S(1)}, u32[]{:S(2)}, u32[]{:S(2)}) async-start(f32[32,8,4,128]{3,2,1,0:T(4,128)} %bitcast.38), calls=%async_computation.1 | async-start | bytes 1048576 | tf_op jit(solution)/shard_map/all_to_all | solution.py:224
  63.9 20.8 %copy-start.5 = (bf16[4,128,128]{2,1,0:T(8,128)(2,1)S(1)}, bf16[4,128,128]{2,1,0:T(8,128)(2,1)}, u32[]{:S(2)}) copy-start(bf16[4,128,128]{2,1,0:T(8,128)(2,1)} %param.9) | copy-start | bytes 393220
  86.3 20.5 %copy-start.2 = (f32[8,4,32,128]{3,2,1,0:T(8,128)S(1)}, f32[8,4,32,128]{3,2,1,0:T(8,128)}, u32[]{:S(2)}) copy-start(f32[8,4,32,128]{3,2,1,0:T(8,128)} %get-tuple-element.3) | copy-start | bytes 1572868
  102.2 14.1 %all-to-all-start.4 = ((f32[32,8,384]{2,1,0:T(8,128)}), f32[32,8,384]{2,1,0:T(8,128)S(1)}, u32[]{:S(2)}, u32[]{:S(2)}) async-start(f32[32,8,384]{2,1,0:T(8,128)} %broadcast_in_dim.10), calls=%async_computation.4 | async-start | bytes 786432 | tf_op jit(solution)/shard_map/all_to_all | solution.py:141
  134.9 5.2 %copy-start.4 = (f32[128,128]{1,0:T(8,128)S(1)}, f32[128,128]{1,0:T(8,128)}, u32[]{:S(2)}) copy-start(f32[128,128]{1,0:T(8,128)} %fusion.95) | copy-start | bytes 196612
  142.5 3.2 %copy-start.1 = (f32[128,256]{1,0:T(8,128)S(1)}, f32[128,256]{1,0:T(8,128)}, u32[]{:S(2)}) copy-start(f32[128,256]{1,0:T(8,128)} %shard_map.86) | copy-start | bytes 393220
